TPU v7x, 32 devices: a whole 2x2x4 slice. The times are simulated.
32 devices in a mesh: slab: 2 (over x), row: 8 (over z, y), col: 2 (over core).
Axes of the slice: x: 2, y: 2, z: 4, core: 2. Of those that a mesh axis runs over, the one named last changes fastest.
Arguments:
- features: bfloat16 [256, 512, 256], P(('slab', 'row'), 'col'), parts along dimension 0, may hold values from -6 to 6
- teacher: bfloat16 [256, 512, 256], P(('slab', 'row'), 'col'), parts along dimension 0, may hold values from -6 to 6
- kernel_horiz: float32 [31, 256], replicated, may hold values from -1 to 1
- kernel_vert: float32 [31, 256], replicated, may hold values from -1 to 1
- norm_gain_vector: float32 [256], replicated, may hold values from 0.25 to 1.75
- weight_in: bfloat16 [256, 1024], replicated, may hold values from -0.375 to 0.375
- weight_out: bfloat16 [1024, 256], replicated, may hold values from -0.1875 to 0.1875
Outputs:
- student: bfloat16 [256, 512, 256], P(('slab', 'row'), 'col'), parts along dimension 0
- grad_features: bfloat16 [256, 512, 256], P(('slab', 'row'), 'col'), parts along dimension 0
- grad_in: float32 [512, 1024], P('slab'), parts along dimension 0
- grad_out: float32 [2048, 256], P('slab'), parts along dimension 0
- grad_horiz: float32 [62, 256], P('slab'), parts along dimension 0
- grad_vert: float32 [62, 256], P('slab'), parts along dimension 0
- gain_gradient: float32 [512], P('slab'), parts along dimension 0
There are 2 independent parts, one for each index of `slab`. A program takes and returns all parts, laid end to end along the dimension named above; an argument that names none is the same for every part. Nothing has to cross between parts.
All inputs are finite; a program needn't handle non-finite values.
Results may differ from a plain program's by a relative error of at most 0.0061.
Values may be sent and summed in bfloat16 or wider, within the bound.
No kernel may reach another device: no remote copies, remote signals or barrier semaphores. Data moves between devices by JAX's collectives and lax.ppermute only.
A program may use at most 128 MiB of HBM per device.

v0:
```python
import jax
import jax.numpy as jnp
from jax import lax
from jax.sharding import PartitionSpec as P

root_half = 0.7071067811865476
inv_root_two_pi = 0.3989422804014327


def extended(x, sides, width):
    for axis, dim in sides:
        size, length = (lax.axis_size(axis), x.shape[dim])
        up = [(i, (i + 1) % size) for i in range(size - 1)]
        down = [(j, i) for i, j in up]
        last = lax.slice_in_dim(x, length - width, length, axis=dim)
        initial = lax.slice_in_dim(x, 0, width, axis=dim)
        before = lax.ppermute(last, axis, up)
        after = lax.ppermute(initial, axis, down)
        x = jnp.concatenate([before, x, after], axis=dim)
    return x


def horizontal(padded, kernel, count):
    total = jnp.zeros((padded.shape[0], count, padded.shape[2]), jnp.float32)
    for offset in range(kernel.shape[0]):
        total = total + kernel[offset] * padded[:, offset : offset + count, :]
    return total


def vertical(padded, kernel, count):
    total = jnp.zeros((count, padded.shape[1], padded.shape[2]), jnp.float32)
    for offset in range(kernel.shape[0]):
        total = total + kernel[offset] * padded[offset : offset + count, :, :]
    return total


def tap_sums(left, padded, reduce_dimension):
    length = left.shape[reduce_dimension]
    wide = left.astype(jnp.float32)
    rows_out = []
    for offset in range(padded.shape[reduce_dimension] - length + 1):
        window = lax.slice_in_dim(padded, offset, offset + length, axis=reduce_dimension)
        rows_out.append(jnp.sum(wide * window.astype(jnp.float32), axis=(0, 1)))
    return jnp.stack(rows_out)


def pointwise(features, mixed, teacher, norm_gain_vector, weight_in, weight_out):
    shape = features.shape
    chans = shape[-1]
    summed_in = features.astype(jnp.float32).reshape(-1, chans) + mixed.reshape(-1, chans)
    centre = jnp.mean(summed_in, axis=-1, keepdims=True)
    mean_removed = summed_in - centre
    spread = jnp.mean(mean_removed * mean_removed, axis=-1, keepdims=True)
    inverse_deviation = lax.rsqrt(spread + 1e-06)
    standardized_input = mean_removed * inverse_deviation
    normalized_input = (standardized_input * norm_gain_vector).astype(jnp.bfloat16)
    pre = jnp.dot(normalized_input, weight_in, preferred_element_type=jnp.float32)
    cdf = 0.5 * (1.0 + lax.erf(pre * root_half))
    activ = (pre * cdf).astype(jnp.bfloat16)
    total = summed_in + jnp.dot(activ, weight_out, preferred_element_type=jnp.float32)
    student = total.astype(jnp.bfloat16)
    feature_residual = (total - teacher.astype(jnp.float32).reshape(-1, chans)).astype(jnp.bfloat16)
    grad_out = lax.dot_general(
        activ, feature_residual, (((0,), (0,)), ((), ())), preferred_element_type=jnp.float32
    )
    back_act = lax.dot_general(
        feature_residual, weight_out, (((1,), (1,)), ((), ())), preferred_element_type=jnp.float32
    )
    slope = cdf + pre * jnp.exp(-0.5 * pre * pre) * inv_root_two_pi
    back_pre = (back_act * slope).astype(jnp.bfloat16)
    grad_in = lax.dot_general(
        normalized_input, back_pre, (((0,), (0,)), ((), ())), preferred_element_type=jnp.float32
    )
    norm_backward = lax.dot_general(
        back_pre, weight_in, (((1,), (1,)), ((), ())), preferred_element_type=jnp.float32
    )
    gain_gradient = jnp.sum(norm_backward * standardized_input, axis=0)
    gain_scaled = norm_backward * norm_gain_vector
    backward_total = feature_residual.astype(jnp.float32) + inverse_deviation * (
        gain_scaled
        - jnp.mean(gain_scaled, axis=-1, keepdims=True)
        - standardized_input * jnp.mean(gain_scaled * standardized_input, axis=-1, keepdims=True)
    )
    backward_total = backward_total.astype(jnp.bfloat16)
    return (student.reshape(shape), backward_total.reshape(shape), grad_in, grad_out, gain_gradient)


def on_device(
    features, teacher, kernel_horiz, kernel_vert, norm_gain_vector, weight_in, weight_out
):
    rows_here = features.shape[0]
    cols_here = features.shape[1]
    margin = (kernel_horiz.shape[0] - 1) // 2
    padded_x = extended(features, (("col", 1),), margin)
    first = horizontal(padded_x, kernel_horiz, cols_here).astype(jnp.bfloat16)
    padded_first = extended(first, (("row", 0),), margin)
    second = vertical(padded_first, kernel_vert, rows_here)
    student, backward_total, grad_in, grad_out, gain_gradient = pointwise(
        features, second, teacher, norm_gain_vector, weight_in, weight_out
    )
    grad_vert = tap_sums(backward_total, padded_first, 0)
    padded_back = extended(backward_total, (("row", 0),), margin)
    back_first = vertical(padded_back, kernel_vert[::-1], rows_here).astype(jnp.bfloat16)
    padded_bf = extended(back_first, (("col", 1),), margin)
    grad_horiz = tap_sums(back_first, padded_x, 1)
    grad_features = (
        backward_total.astype(jnp.float32) + horizontal(padded_bf, kernel_horiz[::-1], cols_here)
    ).astype(jnp.bfloat16)
    totals = lax.psum((grad_in, grad_out, grad_horiz, grad_vert, gain_gradient), ("row", "col"))
    cells = rows_here * lax.axis_size("row") * cols_here * lax.axis_size("col")
    factor = 1.0 / jnp.sqrt(jnp.float32(cells))
    return (
        student,
        grad_features,
        totals[0] * factor,
        totals[1] * factor,
        totals[2] * factor,
        totals[3] * factor,
        totals[4] * factor,
    )


def solution(mesh):
    return jax.shard_map(
        on_device,
        mesh=mesh,
        in_specs=(
            P(("slab", "row"), "col", None),
            P(("slab", "row"), "col", None),
            P(),
            P(),
            P(),
            P(),
            P(),
        ),
        out_specs=(
            P(("slab", "row"), "col", None),
            P(("slab", "row"), "col", None),
            P("slab", None),
            P("slab", None),
            P("slab", None),
            P("slab", None),
            P("slab"),
        ),
        check_vma=False,
    )
```

profile of v0, /device:TPU:0, one launch (start us, length us, event | category | flops | bytes accessed | tf_op | source)
XLA Modules:
  0.0 555.3 jit_solution(1855506094057422923)
XLA Ops:
  7.2 0.0 copy-start
  7.2 0.0 all-reduce.4.cloned.1.call-start
  7.2 0.0 copy-start.9
  7.2 1.2 fusion.269
  8.4 2.4 collective-permute-start
  10.8 1.3 collective-permute-start.1
  12.1 1.0 fusion.273
  13.1 1.0 fusion.272
  14.1 1.7 constant_dynamic-update-slice_fusion.1
  15.9 17.6 %fusion.36 = bf16[16,256,256]{2,1,0:T(8,128)(2,1)S(1)} fusion(bf16[16,256,256]{2,1,0:T(8,128)(2,1)S(1)} %copy-done.9, bf16[16,15,256]{2,1,0:T(8,128)(2,1)S(1)} %collective-permute-done, f32[256]{0:T(256)S(1)} %bitcast.285, f32[256]{0:T(256)S(1)} %bitcast.287, f32[256]{0:T(256)S(1)} %bitcast.291, f32[256]{0:T(256)S(1)} %bitcast.293, f32[256]{0:T(256)S(1)} %bitcast.295, ...), kind=kLoop, calls=%fused_computation.322 | loop fusion | flops 144703488 | bytes 35806208 | tf_op jit(solution)/shard_map/convert_element_type | solution.py:95
  33.5 0.4 fusion.268
  34.0 1.3 collective-permute-start.3
  35.3 5.2 collective-permute-start.2
  40.5 40.9 %collective-permute-done.3 = bf16[15,256,256]{2,1,0:T(8,128)(2,1)S(1)} collective-permute-done((bf16[15,256,256]{2,1,0:T(8,128)(2,1)S(1)}, bf16[15,256,256]{2,1,0:T(8,128)(2,1)S(1)}, u32[]{:S(2)}, u32[]{:S(2)}) %collective-permute-start.3) | collective-permute-done | bytes 1966112 | tf_op jit(solution)/shard_map/ppermute | solution.py:18
  81.4 43.0 %collective-permute-done.2 = bf16[15,256,256]{2,1,0:T(8,128)(2,1)S(1)} collective-permute-done((bf16[15,256,256]{2,1,0:T(8,128)(2,1)S(1)}, bf16[15,256,256]{2,1,0:T(8,128)(2,1)S(1)}, u32[]{:S(2)}, u32[]{:S(2)}) %collective-permute-start.2) | collective-permute-done | bytes 1966112 | tf_op jit(solution)/shard_map/ppermute | solution.py:17
  124.4 57.0 %fusion.265 = (f32[16,256]{1,0:T(8,128)S(1)}, f32[16,256,256]{2,1,0:T(8,128)S(1)}) fusion(bf16[15,256,256]{2,1,0:T(8,128)(2,1)S(1)} %collective-permute-done.3, bf16[16,256,256]{2,1,0:T(8,128)(2,1)S(1)} %fusion.36, f32[256]{0:T(256)S(1)} %bitcast.223, f32[256]{0:T(256)S(1)} %bitcast.225, f32[256]{0:T(256)S(1)} %bitcast.229, f32[256]{0:T(256)S(1)} %bitcast.231, ...), kind=kLoop, calls=%fused_computation.593 | loop fusion | flops 131067904 | bytes 12368896 | tf_op jit(solution)/shard_map/reduce_sum | solution.py:51
  181.5 1.3 multiply_reduce_fusion.2
  182.9 2.3 multiply_convert_fusion.1
  185.3 8.4 %multiply_convert_fusion = (bf16[4096,1024]{1,0:T(8,128)(2,1)S(1)}, f32[4096,1024]{1,0:T(8,128)}) fusion(bf16[4096,256]{1,0:T(8,128)(2,1)S(1)} %multiply_convert_fusion.1, bf16[256,1024]{1,0:T(8,128)(2,1)S(1)} %copy-done), kind=kOutput, calls=%fused_computation.72 | convolution fusion | flops 2168455168 | bytes 27787264 | tf_op jit(solution)/shard_map/dot_general | solution.py:57
  193.6 4.2 fusion.161
  197.8 12.9 %fusion.5 = bf16[4096,1024]{1,0:T(8,128)(2,1)S(1)} fusion(f32[4096,1024]{1,0:T(8,128)} %get-tuple-element.156, bf16[4096,256]{1,0:T(8,128)(2,1)S(1)} %get-tuple-element.81, bf16[1024,256]{1,0:T(8,128)(2,1)S(1)} %copy-done.18), kind=kOutput, calls=%fused_computation.71 | convolution fusion | flops 2189426688 | bytes 27787264 | tf_op jit(solution)/shard_map/dot_general | solution.py:66
  210.8 5.7 %multiply_reduce_fusion = (f32[256]{0:T(256)}, f32[4096]{0:T(1024)S(1)}, f32[4096]{0:T(1024)S(1)}, f32[4096,256]{1,0:T(8,128)}) fusion(f32[16,256,256]{2,1,0:T(8,128)S(1)} %get-tuple-element.80, f32[4096]{0:T(1024)S(1)} %bitcast.198, f32[4096]{0:T(1024)S(1)} %bitcast.201, f32[256]{0:T(256)S(1)} %copy-done.20, bf16[4096,1024]{1,0:T(8,128)(2,1)S(1)} %fusion.5, ...), kind=kOutput, calls=%fused_computation.451 | convolution fusion | flops 2155863808 | bytes 17369088 | tf_op jit(solution)/shard_map/dot_general | solution.py:74
  216.5 3.3 fusion.274
  219.8 3.4 fusion.275
  223.2 20.6 %fusion.160 = (f32[256]{0:T(256)S(1)}, f32[256]{0:T(256)S(1)}, f32[256]{0:T(256)S(1)}, f32[256]{0:T(256)S(1)}, f32[256]{0:T(256)S(1)}, /*index=5*/f32[256]{0:T(2...) fusion(bf16[15,256,256]{2,1,0:T(8,128)(2,1)} %copy-done.15, ...), kind=kLoop, calls=%fused_computation.446 | loop fusion | flops 49280768 | bytes 16721920 | tf_op jit(solution)/shard_map/reduce_sum | solution.py:43
  243.9 1.3 copy-done.2
  245.2 2.2 fusion.267
  247.4 1.3 collective-permute-start.5
  248.7 6.4 %collective-permute-start.4 = (bf16[15,256,256]{2,1,0:T(8,128)(2,1)}, bf16[15,256,256]{2,1,0:T(8,128)(2,1)}, u32[]{:S(2)}, u32[]{:S(2)}) collective-permute-start(bf16[15,256,256]{2,1,0:T(8,128)(2,1)} %bitcast.66), channel_id=1, source_target_pairs={{0,2},{2,4},{4,6},{6,8},{8,10},{10,12},{12,14},{1,3},{3,5},{5,7},{... | collective-permute-start | bytes 5898248 | tf_op jit(solution)/shard_map/ppermute | solution.py:17
  255.1 0.0 all-reduce.4.cloned.1.call-update
  255.1 10.5 %fusion.144 = (f32[256]{0:T(256)S(1)}, f32[256]{0:T(256)S(1)}, f32[256]{0:T(256)S(1)}, f32[256]{0:T(256)S(1)}, f32[256]{0:T(256)S(1)}, /*index=5*/f32[256]{0:T(2...) fusion(bf16[16,256,256]{2,1,0:T(8,128)(2,1)} %copy-done.6, bf16[15,256,256]{2,1,0:T(8,128)(2,1)} %copy-done.13, ...), kind=kLoop, calls=%fused_computation.430 | loop fusion | flops 38795008 | bytes 6169600 | tf_op jit(solution)/shard_map/reduce_sum | solution.py:43
  265.6 3.4 fusion.159
  269.1 2.8 fusion.143
  271.9 0.1 stack.255
  272.0 121.9 %all-reduce.4.cloned.1.call-done = (f32[256,1024]{1,0:T(8,128)}, f32[1024,256]{1,0:T(8,128)}) async-done(((f32[256,1024]{1,0:T(8,128)}, f32[1024,256]{1,0:T(8,128)}), (f32[256,1024]{1,0:T(8,128)}, f32[1024,256]{1,0:T(8,128)})) %all-reduce.4.cloned.1.call-update) | async-done | bytes 2097168 | tf_op jit(solution)/shard_map/psum | solution.py:109
  393.8 2.5 broadcast_multiply_fusion.1
  396.3 2.3 broadcast_multiply_fusion
  398.6 31.3 %fusion.113 = (f32[256]{0:T(256)S(1)}, f32[256]{0:T(256)S(1)}, f32[256]{0:T(256)S(1)}, f32[256]{0:T(256)S(1)}, f32[256]{0:T(256)S(1)}, /*index=5*/f32[256]{0:T(2...) fusion(bf16[16,271,256]{2,1,0:T(8,128)(2,1)S(1)} %constant_dyna, ...), kind=kLoop, calls=%fused_computation.399 | loop fusion | flops 177205504 | bytes 39630848 | tf_op jit(solution)/shard_map/reduce_sum | solution.py:43
  429.9 1.3 collective-permute-start.7
  431.2 3.2 collective-permute-start.6
  434.4 4.6 fusion.96
  439.1 5.9 %fusion.97 = (f32[256]{0:T(256)S(1)}, f32[256]{0:T(256)S(1)}, f32[256]{0:T(256)S(1)}, f32[256]{0:T(256)S(1)}, f32[256]{0:T(256)S(1)}, /*index=5*/f32[256]{0:T(256)S(1)}, f32[256]{0:T(256)S(1)}, f32[256]{0:T(256)}, f32[256]{0:T(256)}) fusion(bf16[16,256,256]{2,1,0:T(8,128)(2,1)S(1)} %get-tuple-element.78, bf16[16,256,256]{2,1,0:T(8,128)(2,1)S(1)} %copy-done.10, ...), kind=kLoop, calls=%fused_computation.383 | loop fusion | flops 57669376 | bytes 4326400 | tf_op jit(solution)/shard_map/reduce_sum | solution.py:43
  445.0 0.8 stack.223
  445.8 60.4 %all-reduce = (f32[31,256]{1,0:T(8,128)S(1)}, f32[31,256]{1,0:T(8,128)S(1)}, f32[256]{0:T(256)S(1)}) all-reduce(f32[31,256]{1,0:T(8,128)S(1)} %stack.223, f32[31,256]{1,0:T(8,128)S(1)} %stack.255, f32[256]{0:T(256)} %get-tuple-element.7), channel_id=1, replica_groups=mesh['slab'=2,'row'=8,'col'=2] {'row','col'}, use_global_device_ids=true, to_apply=%region_37.0 | all-reduce | flops 16128 | bytes 129024 | tf_op jit(solution)/shard_map/psum | solution.py:109
  506.2 0.6 broadcast_multiply_fusion.3
  506.8 0.6 broadcast_multiply_fusion.2
  507.5 0.6 broadcast_multiply_fusion.7
  508.0 40.4 %fusion.164 = bf16[16,256,256]{2,1,0:T(8,128)(2,1)} fusion(bf16[16,256,256]{2,1,0:T(8,128)(2,1)} %copy-done.11, bf16[16,15,256]{2,1,0:T(8,128)(2,1)S(1)} %collective-permute-done.7, bf16[16,15,256]{2,1,0:T(8,128)(2,1)S(1)} %collective-permute-done.6, f32[256]{0:T(256)S(1)} %bitcast.286, f32[256]{0:T(256)S(1)} %bitcast.288, f32[256]{0:T(256)S(1)} %bitcast.292, ...), kind=kLoop, calls=%fused_computation.457 | loop fusion | flops 193986560 | bytes 6568960 | tf_op jit(solution)/shard_map/convert_element_type | solution.py:108
  (54 shorter events, 0.2 us)
Async XLA Ops:
  7.2 178.1 %copy-start = (bf16[256,1024]{1,0:T(8,128)(2,1)S(1)}, bf16[256,1024]{1,0:T(8,128)(2,1)}, u32[]{:S(2)}) copy-start(bf16[256,1024]{1,0:T(8,128)(2,1)} %param.12) | copy-start | bytes 1572868
  7.2 386.6 %all-reduce.4.cloned.1.call-start = ((), (), s32[]{:S(2)}) async-start(), calls=%async_computation | async-start | bytes 4194304 | tf_op jit(solution)/shard_map/psum | solution.py:109
  7.2 8.7 %copy-start.9 = (bf16[16,256,256]{2,1,0:T(8,128)(2,1)S(1)}, bf16[16,256,256]{2,1,0:T(8,128)(2,1)}, u32[]{:S(2)}) copy-start(bf16[16,256,256]{2,1,0:T(8,128)(2,1)} %param.7) | copy-start | bytes 6291460
  8.4 7.5 %collective-permute-start = (bf16[16,15,256]{2,1,0:T(8,128)(2,1)S(1)}, bf16[16,15,256]{2,1,0:T(8,128)(2,1)S(1)}, u32[]{:S(2)}, u32[]{:S(2)}) collective-permute-start(bf16[16,15,256]{2,1,0:T(8,128)(2,1)S(1)} %get-tuple-element.90), channel_id=1, source_target_pairs={{0,1},{2,3},{4,5},{6,7},{8,9},{10,11},{12,13},{14,15},{16,17},{18,... | collective-permute-start | bytes 368648 | tf_op jit(solution)/shard_map/ppermute | solution.py:17
  10.8 5.0 collective-permute-start.1
  33.5 148.0 %copy-start.6 = (bf16[16,256,256]{2,1,0:T(8,128)(2,1)}, bf16[16,256,256]{2,1,0:T(8,128)(2,1)S(1)}, u32[]{:S(2)}) copy-start(bf16[16,256,256]{2,1,0:T(8,128)(2,1)S(1)} %fusion.36) | copy-start | bytes 6291460
  33.5 6.9 %copy-start.19 = (f32[31,256]{1,0:T(8,128)S(1)}, f32[31,256]{1,0:T(8,128)}, u32[]{:S(2)}) copy-start(f32[31,256]{1,0:T(8,128)} %param.10) | copy-start | bytes 95236
  34.0 47.5 %collective-permute-start.3 = (bf16[15,256,256]{2,1,0:T(8,128)(2,1)S(1)}, bf16[15,256,256]{2,1,0:T(8,128)(2,1)S(1)}, u32[]{:S(2)}, u32[]{:S(2)}) collective-permute-start(bf16[15,256,256]{2,1,0:T(8,128)(2,1)S(1)} %get-tuple-element.88), channel_id=1, source_target_pairs={{2,0},{4,2},{6,4},{8,6},{10,8},{12,10},{14,12},{3,1},{5,3},{7,5},{... | collective-permute-start | bytes 5898248 | tf_op jit(solution)/shard_map/ppermute | solution.py:18
  35.3 89.2 %collective-permute-start.2 = (bf16[15,256,256]{2,1,0:T(8,128)(2,1)S(1)}, bf16[15,256,256]{2,1,0:T(8,128)(2,1)S(1)}, u32[]{:S(2)}, u32[]{:S(2)}) collective-permute-start(bf16[15,256,256]{2,1,0:T(8,128)(2,1)S(1)} %get-tuple-element.87), channel_id=1, source_target_pairs={{0,2},{2,4},{4,6},{6,8},{8,10},{10,12},{12,14},{1,3},{3,5},{5,7},{... | collective-permute-start | bytes 5898248 | tf_op jit(solution)/shard_map/ppermute | solution.py:17
  81.4 100.0 %copy-start.15 = (bf16[15,256,256]{2,1,0:T(8,128)(2,1)}, bf16[15,256,256]{2,1,0:T(8,128)(2,1)S(1)}, u32[]{:S(2)}) copy-start(bf16[15,256,256]{2,1,0:T(8,128)(2,1)S(1)} %collective-permute-done.3) | copy-start | bytes 5898244
  124.4 57.0 %copy-start.13 = (bf16[15,256,256]{2,1,0:T(8,128)(2,1)}, bf16[15,256,256]{2,1,0:T(8,128)(2,1)S(1)}, u32[]{:S(2)}) copy-start(bf16[15,256,256]{2,1,0:T(8,128)(2,1)S(1)} %collective-permute-done.2) | copy-start | bytes 5898244
  181.5 29.3 %copy-start.8 = (f32[16,256,256]{2,1,0:T(8,128)}, f32[16,256,256]{2,1,0:T(8,128)S(1)}, u32[]{:S(2)}) copy-start(f32[16,256,256]{2,1,0:T(8,128)S(1)} %get-tuple-element.80) | copy-start | bytes 12582916
  181.5 1.4 copy-start.20
  185.2 8.4 %copy-start.17 = (bf16[16,256,256]{2,1,0:T(8,128)(2,1)S(1)}, bf16[16,256,256]{2,1,0:T(8,128)(2,1)}, u32[]{:S(2)}) copy-start(bf16[16,256,256]{2,1,0:T(8,128)(2,1)} %param.8) | copy-start | bytes 6291460
  185.2 8.4 %copy-start.18 = (bf16[1024,256]{1,0:T(8,128)(2,1)S(1)}, bf16[1024,256]{1,0:T(8,128)(2,1)}, u32[]{:S(2)}) copy-start(bf16[1024,256]{1,0:T(8,128)(2,1)} %param.13) | copy-start | bytes 1572868
  197.8 22.0 %copy-start.12 = (bf16[4096,256]{1,0:T(8,128)(2,1)}, bf16[4096,256]{1,0:T(8,128)(2,1)S(1)}, u32[]{:S(2)}) copy-start(bf16[4096,256]{1,0:T(8,128)(2,1)S(1)} %get-tuple-element.81) | copy-start | bytes 6291460
  243.9 1.4 copy-start.2
  247.4 151.2 %collective-permute-start.5 = (bf16[15,256,256]{2,1,0:T(8,128)(2,1)}, bf16[15,256,256]{2,1,0:T(8,128)(2,1)}, u32[]{:S(2)}, u32[]{:S(2)}) collective-permute-start(bf16[15,256,256]{2,1,0:T(8,128)(2,1)} %bitcast.67), channel_id=1, source_target_pairs={{2,0},{4,2},{6,4},{8,6},{10,8},{12,10},{14,12},{3,1},{5,3},{7,5},{... | collective-permute-start | bytes 5898248 | tf_op jit(solution)/shard_map/ppermute | solution.py:18
  248.7 149.9 %collective-permute-start.4 = (bf16[15,256,256]{2,1,0:T(8,128)(2,1)}, bf16[15,256,256]{2,1,0:T(8,128)(2,1)}, u32[]{:S(2)}, u32[]{:S(2)}) collective-permute-start(bf16[15,256,256]{2,1,0:T(8,128)(2,1)} %bitcast.66), channel_id=1, source_target_pairs={{0,2},{2,4},{4,6},{6,8},{8,10},{10,12},{12,14},{1,3},{3,5},{5,7},{... | collective-permute-start | bytes 5898248 | tf_op jit(solution)/shard_map/ppermute | solution.py:17
  255.1 10.5 %copy-start.3 = (bf16[4096,256]{1,0:T(8,128)(2,1)S(1)}, bf16[4096,256]{1,0:T(8,128)(2,1)}, u32[]{:S(2)}) copy-start(bf16[4096,256]{1,0:T(8,128)(2,1)} %copy-done.2) | copy-start | bytes 6291460
  255.1 10.5 %copy-start.7 = (bf16[16,256,256]{2,1,0:T(8,128)(2,1)S(1)}, bf16[16,256,256]{2,1,0:T(8,128)(2,1)}, u32[]{:S(2)}) copy-start(bf16[16,256,256]{2,1,0:T(8,128)(2,1)} %copy-done.6) | copy-start | bytes 6291460
  255.1 10.5 %copy-start.16 = (bf16[15,256,256]{2,1,0:T(8,128)(2,1)S(1)}, bf16[15,256,256]{2,1,0:T(8,128)(2,1)}, u32[]{:S(2)}) copy-start(bf16[15,256,256]{2,1,0:T(8,128)(2,1)} %copy-done.15) | copy-start | bytes 5898244
  265.6 3.4 copy-start.14
  393.8 4.7 copy-start.4
  398.6 35.8 %copy-start.10 = (bf16[16,256,256]{2,1,0:T(8,128)(2,1)S(1)}, bf16[16,256,256]{2,1,0:T(8,128)(2,1)}, u32[]{:S(2)}) copy-start(bf16[16,256,256]{2,1,0:T(8,128)(2,1)} %param.7) | copy-start | bytes 6291460
  429.8 15.2 %copy-start.11 = (bf16[16,256,256]{2,1,0:T(8,128)(2,1)}, bf16[16,256,256]{2,1,0:T(8,128)(2,1)S(1)}, u32[]{:S(2)}) copy-start(bf16[16,256,256]{2,1,0:T(8,128)(2,1)S(1)} %get-tuple-element.78) | copy-start | bytes 6291460
  429.9 78.1 %collective-permute-start.7 = (bf16[16,15,256]{2,1,0:T(8,128)(2,1)S(1)}, bf16[16,15,256]{2,1,0:T(8,128)(2,1)S(1)}, u32[]{:S(2)}, u32[]{:S(2)}) collective-permute-start(bf16[16,15,256]{2,1,0:T(8,128)(2,1)S(1)} %get-tuple-element.84), channel_id=1, source_target_pairs={{1,0},{3,2},{5,4},{7,6},{9,8},{11,10},{13,12},{15,14},{17,16},{19,... | collective-permute-start | bytes 368648 | tf_op jit(solution)/shard_map/ppermute | solution.py:18
  431.2 76.8 %copy-start.5 = (bf16[4096,256]{1,0:T(8,128)(2,1)S(1)}, bf16[4096,256]{1,0:T(8,128)(2,1)}, u32[]{:S(2)}) copy-start(bf16[4096,256]{1,0:T(8,128)(2,1)} %copy-done.2) | copy-start | bytes 6291460
  431.2 76.8 %collective-permute-start.6 = (bf16[16,15,256]{2,1,0:T(8,128)(2,1)S(1)}, bf16[16,15,256]{2,1,0:T(8,128)(2,1)S(1)}, u32[]{:S(2)}, u32[]{:S(2)}) collective-permute-start(bf16[16,15,256]{2,1,0:T(8,128)(2,1)S(1)} %get-tuple-element.83), channel_id=1, source_target_pairs={{0,1},{2,3},{4,5},{6,7},{8,9},{10,11},{12,13},{14,15},{16,17},{18,... | collective-permute-start | bytes 368648 | tf_op jit(solution)/shard_map/ppermute | solution.py:17
  439.0 109.4 %copy-start.1 = (bf16[256,1024]{1,0:T(8,128)(2,1)S(1)}, bf16[256,1024]{1,0:T(8,128)(2,1)}, u32[]{:S(2)}) copy-start(bf16[256,1024]{1,0:T(8,128)(2,1)} %param.12) | copy-start | bytes 1572868
Sparse Core Ops, SparseCore 0:
  255.2 138.5 all-reduce.3
where the time goes:
time: 556 us; the launch traced here: 555 us
  waiting for transfers between devices  206 us (37%)
  other arithmetic  204 us (37%)
  blocking collectives  60.4 us (11%)
  matrix products  37.9 us (7%)
  starting transfers between devices  22.3 us (4%)
  between operations  14.6 us (3%)
  local copies, waits for them, and re-layouts  9.94 us (2%)
    psum x1, waiting for transfers between devices, on_device(): lax.psum((grad_in, grad_out, grad_horiz, grad_vert, gain_gradient), ('row...  122 us
    reduce_sum x7, other arithmetic, tap_sums(): rows_out.append(jnp.sum(wide * window.astype(jnp.float32), axis=(0, 1)))  79.1 us
    psum x1, blocking collectives, on_device(): lax.psum((grad_in, grad_out, grad_horiz, grad_vert, gain_gradient), ('row...  60.4 us
    reduce_sum x1, other arithmetic, pointwise(): centre = jnp.mean(summed_in, axis=-1, keepdims=True)  57 us
    ppermute x4, waiting for transfers between devices, extended(): before = lax.ppermute(last, axis, up)  43 us
    ppermute x4, waiting for transfers between devices, extended(): after = lax.ppermute(initial, axis, down)  40.9 us
    convert_element_type x1, other arithmetic, on_device(): grad_features = (backward_total.astype(jnp.float32) + horizontal(padded_b...  40.4 us
    convert_element_type x1, other arithmetic, on_device(): first = horizontal(padded_x, kernel_horiz, cols_here).astype(jnp.bfloat16)  17.6 us
  transfers between devices with their start and end apart: 9, of which 3 were waited for; matrix products, arithmetic and copies ran while one was open for 7% of the time, Pallas kernels for 0%

commit v1 on v0

--- a/solution.py
+++ b/solution.py
@@ -42,6 +42,19 @@
         window = lax.slice_in_dim(padded, offset, offset + length, axis=reduce_dimension)
         rows_out.append(jnp.sum(wide * window.astype(jnp.float32), axis=(0, 1)))
     return jnp.stack(rows_out)
+
+
+def tree_sum(x, axes):
+    for axis in axes:
+        size = lax.axis_size(axis)
+        if size & (size - 1):
+            x = lax.psum(x, axis)
+            continue
+        step = 1
+        while step < size:
+            x = x + lax.ppermute(x, axis, [(i, i ^ step) for i in range(size)])
+            step *= 2
+    return x
 
 
 def pointwise(features, mixed, teacher, norm_gain_vector, weight_in, weight_out):
@@ -106,7 +119,12 @@
     grad_features = (
         backward_total.astype(jnp.float32) + horizontal(padded_bf, kernel_horiz[::-1], cols_here)
     ).astype(jnp.bfloat16)
-    totals = lax.psum((grad_in, grad_out, grad_horiz, grad_vert, gain_gradient), ("row", "col"))
+    big = lax.psum((grad_in, grad_out), ("row", "col"))
+    taps = tree_sum(
+        jnp.concatenate([grad_horiz, grad_vert, gain_gradient[None]], axis=0), ("col", "row")
+    )
+    count = grad_horiz.shape[0]
+    totals = (big[0], big[1], taps[:count], taps[count : 2 * count], taps[2 * count])
     cells = rows_here * lax.axis_size("row") * cols_here * lax.axis_size("col")
     factor = 1.0 / jnp.sqrt(jnp.float32(cells))
     return (

time: 556 us -> 458 us (0.82)
  blocking collectives: 60.4 us -> 0 us
  waiting for transfers between devices: 206 us -> 166 us
    psum x1, waiting for transfers between devices: 122 us -> 7.48 us  [on_device(): big = lax.psum((grad_in, grad_out), ('row', 'col'))]
    psum x1 -> x0, blocking collectives: 60.4 us -> none  [on_device(): lax.psum((grad_in, grad_out, grad_horiz, grad_vert, gain_gradient), ('row...]
    ppermute x4, waiting for transfers between devices: 43 us -> 90 us  [extended(): before = lax.ppermute(last, axis, up)]
    ppermute x4, waiting for transfers between devices: 40.9 us -> 67.4 us  [extended(): after = lax.ppermute(initial, axis, down)]
  transfers between devices with their start and end apart: 9 -> 13, of which waited for: 3 -> 6; matrix products, arithmetic and copies ran while one was open for 7% -> 24% of each run, Pallas kernels for 0% -> 0%
where the time goes in v1:
time: 458 us; the launch traced here: 457 us
  other arithmetic  203 us (44%)
  waiting for transfers between devices  166 us (36%)
  matrix products  37.4 us (8%)
  starting transfers between devices  26.8 us (6%)
  between operations  14.5 us (3%)
  local copies, waits for them, and re-layouts  10.2 us (2%)
    ppermute x4, waiting for transfers between devices, extended(): before = lax.ppermute(last, axis, up)  90 us
    reduce_sum x7, other arithmetic, tap_sums(): rows_out.append(jnp.sum(wide * window.astype(jnp.float32), axis=(0, 1)))  78 us
    ppermute x4, waiting for transfers between devices, extended(): after = lax.ppermute(initial, axis, down)  67.4 us
    reduce_sum x1, other arithmetic, pointwise(): centre = jnp.mean(summed_in, axis=-1, keepdims=True)  57 us
    convert_element_type x1, other arithmetic, on_device(): grad_features = (backward_total.astype(jnp.float32) + horizontal(padded_b...  40.5 us
    convert_element_type x1, other arithmetic, on_device(): first = horizontal(padded_x, kernel_horiz, cols_here).astype(jnp.bfloat16)  17.6 us
    ppermute x4, starting transfers between devices, extended(): before = lax.ppermute(last, axis, up)  17 us
    dot_general x1, matrix products, pointwise(): lax.dot_general(feature_residual, weight_out, (((1,), (1,)), ((), ())), p...  12.9 us
  transfers between devices with their start and end apart: 13, of which 6 were waited for; matrix products, arithmetic and copies ran while one was open for 24% of the time, Pallas kernels for 0%

profile of v1, /device:TPU:0, one launch (start us, length us, event | category | flops | bytes accessed | tf_op | source)
XLA Modules:
  0.0 457.0 jit_solution(3755200190807514171)
XLA Ops:
  7.2 1.2 fusion.269
  8.4 2.4 collective-permute-start
  10.8 1.3 collective-permute-start.1
  12.1 1.0 fusion.273
  13.1 1.0 fusion.272
  14.1 1.7 constant_dynamic-update-slice_fusion.1
  15.9 17.6 %fusion.36 = bf16[16,256,256]{2,1,0:T(8,128)(2,1)S(1)} fusion(bf16[16,256,256]{2,1,0:T(8,128)(2,1)S(1)} %copy-done.8, bf16[16,15,256]{2,1,0:T(8,128)(2,1)S(1)} %collective-permute-done, f32[256]{0:T(256)S(1)} %bitcast.287, f32[256]{0:T(256)S(1)} %bitcast.289, f32[256]{0:T(256)S(1)} %bitcast.293, f32[256]{0:T(256)S(1)} %bitcast.295, f32[256]{0:T(256)S(1)} %bitcast.297, ...), kind=kLoop, calls=%fused_computation.322 | loop fusion | flops 144703488 | bytes 35806208 | tf_op jit(solution)/shard_map/convert_element_type | solution.py:108
  33.5 0.4 fusion.268
  34.0 1.3 collective-permute-start.3
  35.3 5.2 %collective-permute-start.2 = (bf16[15,256,256]{2,1,0:T(8,128)(2,1)S(1)}, bf16[15,256,256]{2,1,0:T(8,128)(2,1)S(1)}, u32[]{:S(2)}, u32[]{:S(2)}) collective-permute-start(bf16[15,256,256]{2,1,0:T(8,128)(2,1)S(1)} %get-tuple-element.84), channel_id=1, source_target_pairs={{0,2},{2,4},{4,6},{6,8},{8,10},{10,12},{12,14},{1,3},{3,5},{5,7},{... | collective-permute-start | bytes 5898248 | tf_op jit(solution)/shard_map/ppermute | solution.py:17
  40.5 40.9 %collective-permute-done.3 = bf16[15,256,256]{2,1,0:T(8,128)(2,1)S(1)} collective-permute-done((bf16[15,256,256]{2,1,0:T(8,128)(2,1)S(1)}, bf16[15,256,256]{2,1,0:T(8,128)(2,1)S(1)}, u32[]{:S(2)}, u32[]{:S(2)}) %collective-permute-start.3) | collective-permute-done | bytes 1966112 | tf_op jit(solution)/shard_map/ppermute | solution.py:18
  81.4 43.0 %collective-permute-done.2 = bf16[15,256,256]{2,1,0:T(8,128)(2,1)S(1)} collective-permute-done((bf16[15,256,256]{2,1,0:T(8,128)(2,1)S(1)}, bf16[15,256,256]{2,1,0:T(8,128)(2,1)S(1)}, u32[]{:S(2)}, u32[]{:S(2)}) %collective-permute-start.2) | collective-permute-done | bytes 1966112 | tf_op jit(solution)/shard_map/ppermute | solution.py:17
  124.4 57.0 %fusion.265 = (f32[16,256]{1,0:T(8,128)S(1)}, f32[16,256,256]{2,1,0:T(8,128)S(1)}) fusion(bf16[15,256,256]{2,1,0:T(8,128)(2,1)S(1)} %collective-permute-done.3, bf16[16,256,256]{2,1,0:T(8,128)(2,1)S(1)} %fusion.36, f32[256]{0:T(256)S(1)} %bitcast.225, f32[256]{0:T(256)S(1)} %bitcast.227, f32[256]{0:T(256)S(1)} %bitcast.231, f32[256]{0:T(256)S(1)} %bitcast.233, ...), kind=kLoop, calls=%fused_computation.593 | loop fusion | flops 131067904 | bytes 12368896 | tf_op jit(solution)/shard_map/reduce_sum | solution.py:64
  181.5 1.3 multiply_reduce_fusion.2
  182.9 2.3 multiply_convert_fusion.1
  185.3 8.4 %multiply_convert_fusion = (bf16[4096,1024]{1,0:T(8,128)(2,1)S(1)}, f32[4096,1024]{1,0:T(8,128)}) fusion(bf16[4096,256]{1,0:T(8,128)(2,1)S(1)} %multiply_convert_fusion.1, bf16[256,1024]{1,0:T(8,128)(2,1)S(1)} %copy-done), kind=kOutput, calls=%fused_computation.72 | convolution fusion | flops 2168455168 | bytes 27787264 | tf_op jit(solution)/shard_map/dot_general | solution.py:70
  193.6 4.2 fusion.161
  197.9 12.9 %fusion.5 = bf16[4096,1024]{1,0:T(8,128)(2,1)S(1)} fusion(f32[4096,1024]{1,0:T(8,128)} %get-tuple-element.155, bf16[4096,256]{1,0:T(8,128)(2,1)S(1)} %get-tuple-element.78, bf16[1024,256]{1,0:T(8,128)(2,1)S(1)} %copy-done.16), kind=kOutput, calls=%fused_computation.71 | convolution fusion | flops 2189426688 | bytes 27787264 | tf_op jit(solution)/shard_map/dot_general | solution.py:79
  210.8 5.2 %multiply_reduce_fusion = (f32[256]{0:T(256)S(1)}, f32[4096]{0:T(1024)S(1)}, f32[4096]{0:T(1024)S(1)}, f32[4096,256]{1,0:T(8,128)}) fusion(f32[16,256,256]{2,1,0:T(8,128)S(1)} %get-tuple-element.77, f32[4096]{0:T(1024)S(1)} %bitcast.200, f32[4096]{0:T(1024)S(1)} %bitcast.203, f32[256]{0:T(256)S(1)} %copy-done.18, bf16[4096,1024]{1,0:T(8,128)(2,1)S(1)} %fusion.5, ...), kind=kOutput, calls=%fused_computation.451 | convolution fusion | flops 2155863808 | bytes 17369088 | tf_op jit(solution)/shard_map/dot_general | solution.py:87
  216.0 3.3 fusion.274
  219.3 3.4 fusion.275
  222.7 20.7 %fusion.160 = (f32[256]{0:T(256)S(1)}, f32[256]{0:T(256)S(1)}, f32[256]{0:T(256)S(1)}, f32[256]{0:T(256)S(1)}, f32[256]{0:T(256)S(1)}, /*index=5*/f32[256]{0:T(2...) fusion(bf16[15,256,256]{2,1,0:T(8,128)(2,1)} %copy-done.14, ...), kind=kLoop, calls=%fused_computation.446 | loop fusion | flops 49280768 | bytes 16721920 | tf_op jit(solution)/shard_map/reduce_sum | solution.py:43
  243.4 1.3 copy-done.2
  244.7 2.2 fusion.267
  246.9 1.3 collective-permute-start.5
  248.2 6.4 %collective-permute-start.4 = (bf16[15,256,256]{2,1,0:T(8,128)(2,1)}, bf16[15,256,256]{2,1,0:T(8,128)(2,1)}, u32[]{:S(2)}, u32[]{:S(2)}) collective-permute-start(bf16[15,256,256]{2,1,0:T(8,128)(2,1)} %bitcast.66), channel_id=1, source_target_pairs={{0,2},{2,4},{4,6},{6,8},{8,10},{10,12},{12,14},{1,3},{3,5},{5,7},{... | collective-permute-start | bytes 5898248 | tf_op jit(solution)/shard_map/ppermute | solution.py:17
  254.6 8.9 %fusion.159 = (f32[256]{0:T(256)S(1)}, f32[256]{0:T(256)S(1)}, f32[256]{0:T(256)S(1)}, f32[256]{0:T(256)S(1)}, f32[256]{0:T(256)S(1)}, /*index=5*/f32[256]{0:T(256)S(1)}, f32[256]{0:T(256)S(1)}) fusion(bf16[4096,256]{1,0:T(8,128)(2,1)} %copy-done.2, bf16[15,256,256]{2,1,0:T(8,128)(2,1)} %copy-done.14, bf16[16,256,256]{2,1,0:T(8,128)(2,1)} %copy-done.5), kind=kLoop, calls=%fused_computation.445 | loop fusion | flops 29358336 | bytes 6167552 | tf_op jit(solution)/shard_map/reduce_sum | solution.py:43
  263.6 2.8 fusion.143
  266.3 4.7 %fusion.144 = (f32[256]{0:T(256)S(1)}, f32[256]{0:T(256)S(1)}, f32[256]{0:T(256)S(1)}, f32[256]{0:T(256)S(1)}, f32[256]{0:T(256)S(1)}, /*index=5*/f32[256]{0:T(2...) fusion(bf16[16,256,256]{2,1,0:T(8,128)(2,1)S(1)} %copy-done.6, bf16[15,256,256]{2,1,0:T(8,128)(2,1)S(1)} %copy-done.13, ...), kind=kLoop, calls=%fused_computation.430 | loop fusion | flops 38795008 | bytes 6169600 | tf_op jit(solution)/shard_map/reduce_sum | solution.py:43
  271.1 26.5 %collective-permute-done.5 = bf16[15,256,256]{2,1,0:T(8,128)(2,1)} collective-permute-done((bf16[15,256,256]{2,1,0:T(8,128)(2,1)}, bf16[15,256,256]{2,1,0:T(8,128)(2,1)}, u32[]{:S(2)}, u32[]{:S(2)}) %collective-permute-start.5) | collective-permute-done | bytes 1966112 | tf_op jit(solution)/shard_map/ppermute | solution.py:18
  297.6 47.0 %collective-permute-done.4 = bf16[15,256,256]{2,1,0:T(8,128)(2,1)} collective-permute-done((bf16[15,256,256]{2,1,0:T(8,128)(2,1)}, bf16[15,256,256]{2,1,0:T(8,128)(2,1)}, u32[]{:S(2)}, u32[]{:S(2)}) %collective-permute-start.4) | collective-permute-done | bytes 1966112 | tf_op jit(solution)/shard_map/ppermute | solution.py:17
  344.6 31.1 %fusion.113 = (f32[256]{0:T(256)S(1)}, f32[256]{0:T(256)S(1)}, f32[256]{0:T(256)S(1)}, f32[256]{0:T(256)S(1)}, f32[256]{0:T(256)S(1)}, /*index=5*/f32[256]{0:T(2...) fusion(bf16[16,271,256]{2,1,0:T(8,128)(2,1)S(1)} %constant_dyna, ...), kind=kLoop, calls=%fused_computation.399 | loop fusion | flops 177205504 | bytes 39630848 | tf_op jit(solution)/shard_map/reduce_sum | solution.py:43
  375.7 5.4 %fusion.97 = (f32[256]{0:T(256)S(1)}, f32[256]{0:T(256)S(1)}, f32[256]{0:T(256)S(1)}, f32[256]{0:T(256)S(1)}, f32[256]{0:T(256)S(1)}, /*index=5*/f32[256]{0:T(25...) fusion(bf16[16,256,256]{2,1,0:T(8,128)(2,1)S(1)} %get-tuple-element.75, bf16[16,256,256]{2,1,0:T(8,128)(2,1)S(1)} %copy-done.9, ...), kind=kLoop, calls=%fused_computation.383 | loop fusion | flops 57669376 | bytes 4326400 | tf_op jit(solution)/shard_map/reduce_sum | solution.py:43
  381.1 4.4 fusion.96
  385.5 0.2 concatenate.151
  385.8 7.5 %all-reduce.3.cloned.1.call-done = (f32[256,1024]{1,0:T(8,128)}, f32[1024,256]{1,0:T(8,128)}) async-done(((f32[256,1024]{1,0:T(8,128)}, f32[1024,256]{1,0:T(8,128)}), (f32[256,1024]{1,0:T(8,128)}, f32[1024,256]{1,0:T(8,128)})) %all-reduce.3.cloned.1.call-update) | async-done | bytes 2097168 | tf_op jit(solution)/shard_map/psum | solution.py:122
  393.3 2.3 broadcast_multiply_fusion.1
  395.6 1.1 collective-permute-start.9
  396.8 1.0 fusion.266
  397.8 1.3 collective-permute-start.7
  399.1 3.0 collective-permute-start.6
  402.2 1.3 collective-permute-start.10
  403.5 2.3 broadcast_multiply_fusion
  405.8 0.7 collective-permute-done.10
  406.5 2.0 collective-permute-start.11
  408.5 40.5 %fusion.164 = bf16[16,256,256]{2,1,0:T(8,128)(2,1)} fusion(bf16[16,256,256]{2,1,0:T(8,128)(2,1)} %copy-done.10, bf16[16,15,256]{2,1,0:T(8,128)(2,1)S(1)} %collective-permute-done.7, bf16[16,15,256]{2,1,0:T(8,128)(2,1)S(1)} %collective-permute-done.6, f32[256]{0:T(256)S(1)} %bitcast.288, f32[256]{0:T(256)S(1)} %bitcast.290, f32[256]{0:T(256)S(1)} %bitcast.294, ...), kind=kLoop, calls=%fused_computation.457 | loop fusion | flops 193986560 | bytes 6568960 | tf_op jit(solution)/shard_map/convert_element_type | solution.py:121
  449.0 0.6 slice_multiply_fusion
  449.6 0.6 slice_multiply_fusion.2
  (59 shorter events, 0.4 us)
Async XLA Ops:
  7.2 178.1 %copy-start = (bf16[256,1024]{1,0:T(8,128)(2,1)S(1)}, bf16[256,1024]{1,0:T(8,128)(2,1)}, u32[]{:S(2)}) copy-start(bf16[256,1024]{1,0:T(8,128)(2,1)} %param.12) | copy-start | bytes 1572868
  7.2 386.1 %all-reduce.3.cloned.1.call-start = ((), (), s32[]{:S(2)}) async-start(), calls=%async_computation | async-start | bytes 4194304 | tf_op jit(solution)/shard_map/psum | solution.py:122
  7.2 8.7 %copy-start.8 = (bf16[16,256,256]{2,1,0:T(8,128)(2,1)S(1)}, bf16[16,256,256]{2,1,0:T(8,128)(2,1)}, u32[]{:S(2)}) copy-start(bf16[16,256,256]{2,1,0:T(8,128)(2,1)} %param.7) | copy-start | bytes 6291460
  8.4 7.5 %collective-permute-start = (bf16[16,15,256]{2,1,0:T(8,128)(2,1)S(1)}, bf16[16,15,256]{2,1,0:T(8,128)(2,1)S(1)}, u32[]{:S(2)}, u32[]{:S(2)}) collective-permute-start(bf16[16,15,256]{2,1,0:T(8,128)(2,1)S(1)} %get-tuple-element.87), channel_id=1, source_target_pairs={{0,1},{2,3},{4,5},{6,7},{8,9},{10,11},{12,13},{14,15},{16,17},{18,... | collective-permute-start | bytes 368648 | tf_op jit(solution)/shard_map/ppermute | solution.py:17
  10.8 5.0 %collective-permute-start.1 = (bf16[16,15,256]{2,1,0:T(8,128)(2,1)S(1)}, bf16[16,15,256]{2,1,0:T(8,128)(2,1)S(1)}, u32[]{:S(2)}, u32[]{:S(2)}) collective-permute-start(bf16[16,15,256]{2,1,0:T(8,128)(2,1)S(1)} %get-tuple-element.86), channel_id=1, source_target_pairs={{1,0},{3,2},{5,4},{7,6},{9,8},{11,10},{13,12},{15,14},{17,16},{19,... | collective-permute-start | bytes 368648 | tf_op jit(solution)/shard_map/ppermute | solution.py:18
  33.5 148.0 %copy-start.5 = (bf16[16,256,256]{2,1,0:T(8,128)(2,1)}, bf16[16,256,256]{2,1,0:T(8,128)(2,1)S(1)}, u32[]{:S(2)}) copy-start(bf16[16,256,256]{2,1,0:T(8,128)(2,1)S(1)} %fusion.36) | copy-start | bytes 6291460
  33.5 6.9 %copy-start.17 = (f32[31,256]{1,0:T(8,128)S(1)}, f32[31,256]{1,0:T(8,128)}, u32[]{:S(2)}) copy-start(f32[31,256]{1,0:T(8,128)} %param.10) | copy-start | bytes 95236
  34.0 47.5 %collective-permute-start.3 = (bf16[15,256,256]{2,1,0:T(8,128)(2,1)S(1)}, bf16[15,256,256]{2,1,0:T(8,128)(2,1)S(1)}, u32[]{:S(2)}, u32[]{:S(2)}) collective-permute-start(bf16[15,256,256]{2,1,0:T(8,128)(2,1)S(1)} %get-tuple-element.85), channel_id=1, source_target_pairs={{2,0},{4,2},{6,4},{8,6},{10,8},{12,10},{14,12},{3,1},{5,3},{7,5},{... | collective-permute-start | bytes 5898248 | tf_op jit(solution)/shard_map/ppermute | solution.py:18
  35.3 89.2 %collective-permute-start.2 = (bf16[15,256,256]{2,1,0:T(8,128)(2,1)S(1)}, bf16[15,256,256]{2,1,0:T(8,128)(2,1)S(1)}, u32[]{:S(2)}, u32[]{:S(2)}) collective-permute-start(bf16[15,256,256]{2,1,0:T(8,128)(2,1)S(1)} %get-tuple-element.84), channel_id=1, source_target_pairs={{0,2},{2,4},{4,6},{6,8},{8,10},{10,12},{12,14},{1,3},{3,5},{5,7},{... | collective-permute-start | bytes 5898248 | tf_op jit(solution)/shard_map/ppermute | solution.py:17
  81.4 100.0 %copy-start.14 = (bf16[15,256,256]{2,1,0:T(8,128)(2,1)}, bf16[15,256,256]{2,1,0:T(8,128)(2,1)S(1)}, u32[]{:S(2)}) copy-start(bf16[15,256,256]{2,1,0:T(8,128)(2,1)S(1)} %collective-permute-done.3) | copy-start | bytes 5898244
  124.4 57.0 %copy-start.12 = (bf16[15,256,256]{2,1,0:T(8,128)(2,1)}, bf16[15,256,256]{2,1,0:T(8,128)(2,1)S(1)}, u32[]{:S(2)}) copy-start(bf16[15,256,256]{2,1,0:T(8,128)(2,1)S(1)} %collective-permute-done.2) | copy-start | bytes 5898244
  181.5 29.3 %copy-start.7 = (f32[16,256,256]{2,1,0:T(8,128)}, f32[16,256,256]{2,1,0:T(8,128)S(1)}, u32[]{:S(2)}) copy-start(f32[16,256,256]{2,1,0:T(8,128)S(1)} %get-tuple-element.77) | copy-start | bytes 12582916
  181.5 1.4 copy-start.18
  185.2 8.4 %copy-start.15 = (bf16[16,256,256]{2,1,0:T(8,128)(2,1)S(1)}, bf16[16,256,256]{2,1,0:T(8,128)(2,1)}, u32[]{:S(2)}) copy-start(bf16[16,256,256]{2,1,0:T(8,128)(2,1)} %param.8) | copy-start | bytes 6291460
  185.3 8.4 %copy-start.16 = (bf16[1024,256]{1,0:T(8,128)(2,1)S(1)}, bf16[1024,256]{1,0:T(8,128)(2,1)}, u32[]{:S(2)}) copy-start(bf16[1024,256]{1,0:T(8,128)(2,1)} %param.13) | copy-start | bytes 1572868
  197.9 21.5 %copy-start.11 = (bf16[4096,256]{1,0:T(8,128)(2,1)}, bf16[4096,256]{1,0:T(8,128)(2,1)S(1)}, u32[]{:S(2)}) copy-start(bf16[4096,256]{1,0:T(8,128)(2,1)S(1)} %get-tuple-element.78) | copy-start | bytes 6291460
  243.4 1.4 copy-start.2
  246.9 50.7 %collective-permute-start.5 = (bf16[15,256,256]{2,1,0:T(8,128)(2,1)}, bf16[15,256,256]{2,1,0:T(8,128)(2,1)}, u32[]{:S(2)}, u32[]{:S(2)}) collective-permute-start(bf16[15,256,256]{2,1,0:T(8,128)(2,1)} %bitcast.67), channel_id=1, source_target_pairs={{2,0},{4,2},{6,4},{8,6},{10,8},{12,10},{14,12},{3,1},{5,3},{7,5},{... | collective-permute-start | bytes 5898248 | tf_op jit(solution)/shard_map/ppermute | solution.py:18
  248.2 96.4 %collective-permute-start.4 = (bf16[15,256,256]{2,1,0:T(8,128)(2,1)}, bf16[15,256,256]{2,1,0:T(8,128)(2,1)}, u32[]{:S(2)}, u32[]{:S(2)}) collective-permute-start(bf16[15,256,256]{2,1,0:T(8,128)(2,1)} %bitcast.66), channel_id=1, source_target_pairs={{0,2},{2,4},{4,6},{6,8},{8,10},{10,12},{12,14},{1,3},{3,5},{5,7},{... | collective-permute-start | bytes 5898248 | tf_op jit(solution)/shard_map/ppermute | solution.py:17
  254.6 9.0 %copy-start.3 = (bf16[4096,256]{1,0:T(8,128)(2,1)S(1)}, bf16[4096,256]{1,0:T(8,128)(2,1)}, u32[]{:S(2)}) copy-start(bf16[4096,256]{1,0:T(8,128)(2,1)} %copy-done.2) | copy-start | bytes 6291460
  254.6 9.0 %copy-start.6 = (bf16[16,256,256]{2,1,0:T(8,128)(2,1)S(1)}, bf16[16,256,256]{2,1,0:T(8,128)(2,1)}, u32[]{:S(2)}) copy-start(bf16[16,256,256]{2,1,0:T(8,128)(2,1)} %copy-done.5) | copy-start | bytes 6291460
  254.6 9.0 %copy-start.13 = (bf16[15,256,256]{2,1,0:T(8,128)(2,1)S(1)}, bf16[15,256,256]{2,1,0:T(8,128)(2,1)}, u32[]{:S(2)}) copy-start(bf16[15,256,256]{2,1,0:T(8,128)(2,1)} %copy-done.12) | copy-start | bytes 5898244
  344.6 31.2 %copy-start.9 = (bf16[16,256,256]{2,1,0:T(8,128)(2,1)S(1)}, bf16[16,256,256]{2,1,0:T(8,128)(2,1)}, u32[]{:S(2)}) copy-start(bf16[16,256,256]{2,1,0:T(8,128)(2,1)} %param.7) | copy-start | bytes 6291460
  375.7 9.8 %copy-start.10 = (bf16[16,256,256]{2,1,0:T(8,128)(2,1)}, bf16[16,256,256]{2,1,0:T(8,128)(2,1)S(1)}, u32[]{:S(2)}) copy-start(bf16[16,256,256]{2,1,0:T(8,128)(2,1)S(1)} %get-tuple-element.75) | copy-start | bytes 6291460
  381.1 27.4 %copy-start.4 = (bf16[4096,256]{1,0:T(8,128)(2,1)S(1)}, bf16[4096,256]{1,0:T(8,128)(2,1)}, u32[]{:S(2)}) copy-start(bf16[4096,256]{1,0:T(8,128)(2,1)} %copy-done.2) | copy-start | bytes 6291460
  385.7 9.9 %collective-permute-start.8 = (f32[63,256]{1,0:T(8,128)S(1)}, f32[63,256]{1,0:T(8,128)S(1)}, u32[]{:S(2)}, u32[]{:S(2)}) collective-permute-start(f32[63,256]{1,0:T(8,128)S(1)} %concatenate.151), channel_id=1, source_target_pairs={{0,1},{1,0},{2,3},{3,2},{4,5},{5,4},{6,7},{7,6},{8,9},{9,8},{10,11... | collective-permute-start | bytes 193544 | tf_op jit(solution)/shard_map/ppermute | solution.py:55
  395.6 6.5 %collective-permute-start.9 = (f32[63,256]{1,0:T(8,128)S(1)}, f32[63,256]{1,0:T(8,128)S(1)}, u32[]{:S(2)}, u32[]{:S(2)}) collective-permute-start(f32[63,256]{1,0:T(8,128)S(1)} %add.544), channel_id=1, source_target_pairs={{0,2},{2,0},{4,6},{6,4},{8,10},{10,8},{12,14},{14,12},{1,3},{3,1},... | collective-permute-start | bytes 193544 | tf_op jit(solution)/shard_map/ppermute | solution.py:55
  397.8 10.7 %collective-permute-start.7 = (bf16[16,15,256]{2,1,0:T(8,128)(2,1)S(1)}, bf16[16,15,256]{2,1,0:T(8,128)(2,1)S(1)}, u32[]{:S(2)}, u32[]{:S(2)}) collective-permute-start(bf16[16,15,256]{2,1,0:T(8,128)(2,1)S(1)} %get-tuple-element.81), channel_id=1, source_target_pairs={{1,0},{3,2},{5,4},{7,6},{9,8},{11,10},{13,12},{15,14},{17,16},{19,... | collective-permute-start | bytes 368648 | tf_op jit(solution)/shard_map/ppermute | solution.py:18
  399.1 9.4 %collective-permute-start.6 = (bf16[16,15,256]{2,1,0:T(8,128)(2,1)S(1)}, bf16[16,15,256]{2,1,0:T(8,128)(2,1)S(1)}, u32[]{:S(2)}, u32[]{:S(2)}) collective-permute-start(bf16[16,15,256]{2,1,0:T(8,128)(2,1)S(1)} %get-tuple-element.80), channel_id=1, source_target_pairs={{0,1},{2,3},{4,5},{6,7},{8,9},{10,11},{12,13},{14,15},{16,17},{18,... | collective-permute-start | bytes 368648 | tf_op jit(solution)/shard_map/ppermute | solution.py:17
  402.2 4.3 collective-permute-start.10
  403.5 46.7 %copy-start.1 = (bf16[256,1024]{1,0:T(8,128)(2,1)S(1)}, bf16[256,1024]{1,0:T(8,128)(2,1)}, u32[]{:S(2)}) copy-start(bf16[256,1024]{1,0:T(8,128)(2,1)} %param.12) | copy-start | bytes 1572868
  406.5 42.5 %collective-permute-start.11 = (f32[63,256]{1,0:T(8,128)S(1)}, f32[63,256]{1,0:T(8,128)S(1)}, u32[]{:S(2)}, u32[]{:S(2)}) collective-permute-start(f32[63,256]{1,0:T(8,128)S(1)} %add.546), channel_id=1, source_target_pairs={{0,8},{2,10},{4,12},{6,14},{8,0},{10,2},{12,4},{14,6},{1,9},{3,11}... | collective-permute-start | bytes 193544 | tf_op jit(solution)/shard_map/ppermute | solution.py:55
Sparse Core Ops, SparseCore 0:
  254.7 138.5 all-reduce.2

commit v2 on v1

--- a/solution.py
+++ b/solution.py
@@ -104,22 +104,43 @@
     rows_here = features.shape[0]
     cols_here = features.shape[1]
     margin = (kernel_horiz.shape[0] - 1) // 2
+    parts = 4 if cols_here % 32 == 0 else 1
+    width = cols_here // parts
     padded_x = extended(features, (("col", 1),), margin)
-    first = horizontal(padded_x, kernel_horiz, cols_here).astype(jnp.bfloat16)
-    padded_first = extended(first, (("row", 0),), margin)
-    second = vertical(padded_first, kernel_vert, rows_here)
-    student, backward_total, grad_in, grad_out, gain_gradient = pointwise(
-        features, second, teacher, norm_gain_vector, weight_in, weight_out
+    pieces = []
+    for k in range(parts):
+        low = k * width
+        first = horizontal(
+            padded_x[:, low : low + width + 2 * margin], kernel_horiz, width
+        ).astype(jnp.bfloat16)
+        padded_first = extended(first, (("row", 0),), margin)
+        second = vertical(padded_first, kernel_vert, rows_here)
+        student, backward_total, grad_in, grad_out, gain_gradient = pointwise(
+            features[:, low : low + width],
+            second,
+            teacher[:, low : low + width],
+            norm_gain_vector,
+            weight_in,
+            weight_out,
+        )
+        grad_vert = tap_sums(backward_total, padded_first, 0)
+        padded_back = extended(backward_total, (("row", 0),), margin)
+        back_first = vertical(padded_back, kernel_vert[::-1], rows_here).astype(jnp.bfloat16)
+        pieces.append(
+            (student, backward_total, back_first, grad_in, grad_out, gain_gradient, grad_vert)
+        )
+    student = jnp.concatenate([p[0] for p in pieces], axis=1)
+    backward_total = jnp.concatenate([p[1] for p in pieces], axis=1)
+    back_first = jnp.concatenate([p[2] for p in pieces], axis=1)
+    grad_in, grad_out, gain_gradient, grad_vert = (
+        sum(p[i] for p in pieces[1:]) + pieces[0][i] for i in range(3, 7)
     )
-    grad_vert = tap_sums(backward_total, padded_first, 0)
-    padded_back = extended(backward_total, (("row", 0),), margin)
-    back_first = vertical(padded_back, kernel_vert[::-1], rows_here).astype(jnp.bfloat16)
+    big = lax.psum((grad_in, grad_out), ("row", "col"))
     padded_bf = extended(back_first, (("col", 1),), margin)
     grad_horiz = tap_sums(back_first, padded_x, 1)
     grad_features = (
         backward_total.astype(jnp.float32) + horizontal(padded_bf, kernel_horiz[::-1], cols_here)
     ).astype(jnp.bfloat16)
-    big = lax.psum((grad_in, grad_out), ("row", "col"))
     taps = tree_sum(
         jnp.concatenate([grad_horiz, grad_vert, gain_gradient[None]], axis=0), ("col", "row")
     )

time: 458 us -> 475 us (1.037)
  waiting for transfers between devices: 166 us -> 75.5 us
  starting transfers between devices: 26.8 us -> 69.9 us
  other arithmetic: 203 us -> 227 us
  local copies, waits for them, and re-layouts: 10.2 us -> 31.1 us
  matrix products: 37.4 us -> 49.7 us
    ppermute x4 -> x10, waiting for transfers between devices: 67.4 us -> 0.03 us  [extended(): after = lax.ppermute(initial, axis, down)]
    ppermute x4 -> x10, waiting for transfers between devices: 90 us -> 27.9 us  [extended(): before = lax.ppermute(last, axis, up)]
    psum x1, waiting for transfers between devices: 7.48 us -> 45.8 us  [on_device(): big = lax.psum((grad_in, grad_out), ('row', 'col'))]
    ppermute x4 -> x10, starting transfers between devices: 17 us -> 49.8 us  [extended(): before = lax.ppermute(last, axis, up)]
    unnamed x2 -> x4, other arithmetic: 0.01 us -> 31.2 us
    reduce_sum x1 -> x4, other arithmetic: 57 us -> 38.7 us  [pointwise(): centre = jnp.mean(summed_in, axis=-1, keepdims=True)]
    convert_element_type x1, other arithmetic: 40.5 us -> 30.1 us  [on_device(): grad_features = (backward_total.astype(jnp.float32) + horizontal(padded_b...]
    convert_element_type x1 -> x4, other arithmetic: 17.6 us -> 27 us  [on_device(): first = horizontal(padded_x[:, low:low + width + 2 * margin], kernel_hori...]
  transfers between devices with their start and end apart: 13 -> 25, of which waited for: 6 -> 5; matrix products, arithmetic and copies ran while one was open for 24% -> 45% of each run, Pallas kernels for 0% -> 0%
where the time goes in v2:
time: 475 us; the launch traced here: 470 us
  other arithmetic  227 us (48%)
  waiting for transfers between devices  75.5 us (16%)
  starting transfers between devices  69.9 us (15%)
  matrix products  49.7 us (10%)
  local copies, waits for them, and re-layouts  31.1 us (7%)
  between operations  16 us (3%)
    reduce_sum x24, other arithmetic, tap_sums(): rows_out.append(jnp.sum(wide * window.astype(jnp.float32), axis=(0, 1)))  85.1 us
    ppermute x10, starting transfers between devices, extended(): before = lax.ppermute(last, axis, up)  49.8 us
    psum x1, waiting for transfers between devices, on_device(): big = lax.psum((grad_in, grad_out), ('row', 'col'))  45.8 us
    reduce_sum x4, other arithmetic, pointwise(): centre = jnp.mean(summed_in, axis=-1, keepdims=True)  38.7 us
    unnamed x4, other arithmetic  31.2 us
    convert_element_type x1, other arithmetic, on_device(): grad_features = (backward_total.astype(jnp.float32) + horizontal(padded_b...  30.1 us
    ppermute x10, waiting for transfers between devices, extended(): before = lax.ppermute(last, axis, up)  27.9 us
    convert_element_type x4, other arithmetic, on_device(): first = horizontal(padded_x[:, low:low + width + 2 * margin], kernel_hori...  27 us
  transfers between devices with their start and end apart: 25, of which 5 were waited for; matrix products, arithmetic and copies ran while one was open for 45% of the time, Pallas kernels for 0%

profile of v2, /device:TPU:0, one launch (start us, length us, event | category | flops | bytes accessed | tf_op | source)
XLA Modules:
  0.0 469.6 jit_solution(14967079562252261050)
XLA Ops:
  14.3 13.5 %fusion.472 = bf16[16,64,256]{2,1,0:T(8,128)(2,1)S(1)} fusion(bf16[16,256,256]{2,1,0:T(8,128)(2,1)} %param.7, f32[256]{0:T(256)S(1)} %bitcast.788, f32[256]{0:T(256)S(1)} %bitcast.793, f32[256]{0:T(256)S(1)} %bitcast.803, f32[256]{0:T(256)S(1)} %bitcast.808, f32[256]{0:T(256)S(1)} %bitcast.813, f32[256]{0:T(256)S(1)} %bitcast.818, f32[256]{0:T(256)S(1)} %bitcast.823, ...), kind=kLoop, calls=%fused_computation.1294 | loop fusion | flops 24379392 | bytes 16808960 | tf_op jit(solution)/shard_map/convert_element_type | solution.py:115
  27.9 4.3 collective-permute-start.5
  33.6 4.4 fusion.473
  38.2 4.6 collective-permute-start.3
  45.6 4.7 fusion.474
  51.5 5.9 %collective-permute-start.1 = (bf16[15,64,256]{2,1,0:T(8,128)(2,1)}, bf16[15,64,256]{2,1,0:T(8,128)(2,1)}, u32[]{:S(2)}, u32[]{:S(2)}) collective-permute-start(bf16[15,64,256]{2,1,0:T(8,128)(2,1)} %get-tuple-element.230), channel_id=1, source_target_pairs={{0,2},{2,4},{4,6},{6,8},{8,10},{10,12},{12,14},{1,3},{3,5},{5,7},{... | collective-permute-start | bytes 1474568 | tf_op jit(solution)/shard_map/ppermute | solution.py:17
  57.7 4.4 fusion.471
  63.2 11.9 %collective-permute-done.3 = bf16[15,64,256]{2,1,0:T(8,128)(2,1)S(1)} collective-permute-done((bf16[15,64,256]{2,1,0:T(8,128)(2,1)S(1)}, bf16[15,64,256]{2,1,0:T(8,128)(2,1)S(1)}, u32[]{:S(2)}, u32[]{:S(2)}) %collective-permute-start.3) | collective-permute-done | bytes 491552 | tf_op jit(solution)/shard_map/ppermute | solution.py:17
  76.5 5.8 %collective-permute-start.8 = (bf16[15,64,256]{2,1,0:T(8,128)(2,1)}, bf16[15,64,256]{2,1,0:T(8,128)(2,1)}, u32[]{:S(2)}, u32[]{:S(2)}) collective-permute-start(bf16[15,64,256]{2,1,0:T(8,128)(2,1)} %get-tuple-element.236), channel_id=1, source_target_pairs={{0,2},{2,4},{4,6},{6,8},{8,10},{10,12},{12,14},{1,3},{3,5},{5,7},{... | collective-permute-start | bytes 1474568 | tf_op jit(solution)/shard_map/ppermute | solution.py:17
  82.3 4.9 %fusion.719 = (f32[16,64]{1,0:T(8,128)S(1)}, f32[16,64,256]{2,1,0:T(8,128)S(1)}) fusion(bf16[15,64,256]{2,1,0:T(8,128)(2,1)S(1)} %collective-permute-done.4, bf16[16,64,256]{2,1,0:T(8,128)(2,1)S(1)} %fusion.473, f32[256]{0:T(256)S(1)} %bitcast.570, f32[256]{0:T(256)S(1)} %bitcast.578, f32[256]{0:T(256)S(1)} %bitcast.594, f32[256]{0:T(256)S(1)} %bitcast.602, ...), kind=kLoop, calls=%fused_computation.1587 | loop fusion | flops 32766976 | bytes 3116032 | tf_op jit(solution)/shard_map/reduce_sum | solution.py:64
  89.0 5.8 %fusion.720 = (f32[16,64]{1,0:T(8,128)S(1)}, f32[16,64,256]{2,1,0:T(8,128)}) fusion(bf16[15,64,256]{2,1,0:T(8,128)(2,1)S(1)} %collective-permute-done.6, bf16[16,64,256]{2,1,0:T(8,128)(2,1)S(1)} %fusion.472, f32[256]{0:T(256)S(1)} %bitcast.571, f32[256]{0:T(256)S(1)} %bitcast.579, f32[256]{0:T(256)S(1)} %bitcast.595, f32[256]{0:T(256)S(1)} %bitcast.603, ...), kind=kLoop, calls=%fused_computation.1588 | loop fusion | flops 32766976 | bytes 3116032 | tf_op jit(solution)/shard_map/reduce_sum | solution.py:64
  96.7 10.5 %fusion.718 = (f32[16,64]{1,0:T(8,128)S(1)}, f32[16,64,256]{2,1,0:T(8,128)}) fusion(bf16[15,64,256]{2,1,0:T(8,128)(2,1)} %collective-permute-done.2, bf16[16,64,256]{2,1,0:T(8,128)(2,1)} %copy-done.25, f32[256]{0:T(256)S(1)} %bitcast.572, f32[256]{0:T(256)S(1)} %bitcast.580, f32[256]{0:T(256)S(1)} %bitcast.596, f32[256]{0:T(256)S(1)} %bitcast.604, ...), kind=kLoop, calls=%fused_computation.1586 | loop fusion | flops 32766976 | bytes 3116032 | tf_op jit(solution)/shard_map/reduce_sum | solution.py:64
  109.0 8.4 %collective-permute-done.8 = bf16[15,64,256]{2,1,0:T(8,128)(2,1)} collective-permute-done((bf16[15,64,256]{2,1,0:T(8,128)(2,1)}, bf16[15,64,256]{2,1,0:T(8,128)(2,1)}, u32[]{:S(2)}, u32[]{:S(2)}) %collective-permute-start.8) | collective-permute-done | bytes 491552 | tf_op jit(solution)/shard_map/ppermute | solution.py:17
  117.4 17.5 %fusion.721 = (f32[16,64]{1,0:T(8,128)S(1)}, f32[16,64,256]{2,1,0:T(8,128)}) fusion(bf16[15,64,256]{2,1,0:T(8,128)(2,1)} %collective-permute-done.9, bf16[16,64,256]{2,1,0:T(8,128)(2,1)S(1)} %fusion.471, f32[256]{0:T(256)S(1)} %bitcast.573, f32[256]{0:T(256)S(1)} %bitcast.581, f32[256]{0:T(256)S(1)} %bitcast.597, f32[256]{0:T(256)S(1)} %bitcast.605, ...), kind=kLoop, calls=%fused_computation.1589 | loop fusion | flops 32766976 | bytes 3116032 | tf_op jit(solution)/shard_map/reduce_sum | solution.py:64
  142.3 10.1 %fusion.5 = bf16[1024,1024]{1,0:T(8,128)(2,1)S(1)} fusion(f32[1024,1024]{1,0:T(8,128)S(1)} %get-tuple-element.316, bf16[1024,256]{1,0:T(8,128)(2,1)S(1)} %get-tuple-element.220, bf16[1024,256]{1,0:T(8,128)(2,1)S(1)} %copy-done.30), kind=kOutput, calls=%fused_computation.198 | convolution fusion | flops 547356672 | bytes 7340032 | tf_op jit(solution)/shard_map/dot_general | solution.py:79
  168.7 6.5 %fusion.364 = (f32[256]{0:T(256)}, f32[256]{0:T(256)}, f32[256]{0:T(256)}, f32[256]{0:T(256)}, f32[256]{0:T(256)}, /*index=5*/f32[256]{0:T(256)}, f32[256]{0:T(2...) fusion(bf16[15,64,256]{2,1,0:T(8,128)(2,1)} %collective-permute-done.2, ...), kind=kLoop, calls=%fused_computation.1158 | loop fusion | flops 12318464 | bytes 4188160 | tf_op jit(solution)/shard_map/reduce_sum | solution.py:43
  177.6 6.2 %collective-permute-start.13 = (bf16[15,64,256]{2,1,0:T(8,128)(2,1)}, bf16[15,64,256]{2,1,0:T(8,128)(2,1)}, u32[]{:S(2)}, u32[]{:S(2)}) collective-permute-start(bf16[15,64,256]{2,1,0:T(8,128)(2,1)} %bitcast.80), channel_id=1, source_target_pairs={{0,2},{2,4},{4,6},{6,8},{8,10},{10,12},{12,14},{1,3},{3,5},{5,7},{... | collective-permute-start | bytes 1474568 | tf_op jit(solution)/shard_map/ppermute | solution.py:17
  183.7 6.5 %fusion.317 = (f32[256]{0:T(256)S(1)}, f32[256]{0:T(256)S(1)}, f32[256]{0:T(256)S(1)}, f32[256]{0:T(256)}, f32[256]{0:T(256)}, /*index=5*/f32[256]{0:T(256)}, f3...) fusion(bf16[15,64,256]{2,1,0:T(8,128)(2,1)} %collective-permute-done.9, ...), kind=kLoop, calls=%fused_computation.1111 | loop fusion | flops 12318464 | bytes 4188160 | tf_op jit(solution)/shard_map/reduce_sum | solution.py:43
  192.6 6.6 %collective-permute-start.10 = (bf16[15,64,256]{2,1,0:T(8,128)(2,1)}, bf16[15,64,256]{2,1,0:T(8,128)(2,1)}, u32[]{:S(2)}, u32[]{:S(2)}) collective-permute-start(bf16[15,64,256]{2,1,0:T(8,128)(2,1)} %bitcast.78), channel_id=1, source_target_pairs={{0,2},{2,4},{4,6},{6,8},{8,10},{10,12},{12,14},{1,3},{3,5},{5,7},{... | collective-permute-start | bytes 1474568 | tf_op jit(solution)/shard_map/ppermute | solution.py:17
  211.8 6.3 %fusion.411 = (f32[256]{0:T(256)}, f32[256]{0:T(256)}, f32[256]{0:T(256)}, f32[256]{0:T(256)}, f32[256]{0:T(256)}, /*index=5*/f32[256]{0:T(256)}, f32[256]{0:T(2...) fusion(bf16[15,64,256]{2,1,0:T(8,128)(2,1)S(1)} %copy-done.37, bf16[16,64,256]{2,1,0:T(8,128)(2,1)S(1)} %copy-done.19, ...), kind=kLoop, calls=%fused_computation.1205 | loop fusion | flops 12318464 | bytes 4188160 | tf_op jit(solution)/shard_map/reduce_sum | solution.py:43
  220.6 6.7 %fusion.458 = (f32[256]{0:T(256)}, f32[256]{0:T(256)}, f32[256]{0:T(256)}, f32[256]{0:T(256)}, f32[256]{0:T(256)}, /*index=5*/f32[256]{0:T(256)}, f32[256]{0:T(2...) fusion(bf16[15,64,256]{2,1,0:T(8,128)(2,1)S(1)} %copy-done.39, bf16[16,64,256]{2,1,0:T(8,128)(2,1)S(1)} %copy-done.22, ...), kind=kLoop, calls=%fused_computation.1252 | loop fusion | flops 12318464 | bytes 4188160 | tf_op jit(solution)/shard_map/reduce_sum | solution.py:43
  232.9 3.2 fusion.301
  236.8 2.7 fusion.363
  242.1 4.2 fusion.348
  248.5 3.4 fusion.457
  254.6 4.4 fusion.442
  258.9 2.9 stack.571
  261.8 3.3 fusion.410
  265.2 2.6 fusion.394
  267.8 3.7 fusion.395
  271.5 2.9 stack.539
  275.1 3.8 convolution_add_fusion.4
  278.9 4.8 %collective-permute-start.15 = (bf16[15,64,256]{2,1,0:T(8,128)(2,1)}, bf16[15,64,256]{2,1,0:T(8,128)(2,1)S(1)}, u32[]{:S(2)}, u32[]{:S(2)}) collective-permute-start(bf16[15,64,256]{2,1,0:T(8,128)(2,1)} %bitcast.487), channel_id=1, source_target_pairs={{0,2},{2,4},{4,6},{6,8},{8,10},{10,12},{12,14},{1,3},{3,5},{5,7},{... | collective-permute-start | bytes 1474568 | tf_op jit(solution)/shard_map/ppermute | solution.py:17
  285.0 7.9 %constant_dynamic-update-slice_fusion.6 = (bf16[16,271,256]{2,1,0:T(8,128)(2,1)S(1)}, bf16[16,64,256]{2,1,0:T(8,128)(2,1)S(1)}) fusion(bf16[15,64,256]{2,1,0:T(8,128)(2,1)} %collective-permute-done.14, bf16[16,64,256]{2,1,0:T(8,128)(2,1)S(1)} %bitcast.474, f32[256]{0:T(256)S(1)} %bitcast.590, f32[256]{0:T(256)S(1)} %bitcast.494, f32[256]{0:T(256)S(1)} %bitcast.566, ...), kind=kLoop, calls=%fused_computation.1567 | loop fusion | flops 47972352 | bytes 2587648
  293.0 5.6 %collective-permute-start.17 = (bf16[15,64,256]{2,1,0:T(8,128)(2,1)}, bf16[15,64,256]{2,1,0:T(8,128)(2,1)S(1)}, u32[]{:S(2)}, u32[]{:S(2)}) collective-permute-start(bf16[15,64,256]{2,1,0:T(8,128)(2,1)} %bitcast.488), channel_id=1, source_target_pairs={{0,2},{2,4},{4,6},{6,8},{8,10},{10,12},{12,14},{1,3},{3,5},{5,7},{... | collective-permute-start | bytes 1474568 | tf_op jit(solution)/shard_map/ppermute | solution.py:17
  298.6 7.5 %collective-permute-done.15 = bf16[15,64,256]{2,1,0:T(8,128)(2,1)S(1)} collective-permute-done((bf16[15,64,256]{2,1,0:T(8,128)(2,1)}, bf16[15,64,256]{2,1,0:T(8,128)(2,1)S(1)}, u32[]{:S(2)}, u32[]{:S(2)}) %collective-permute-start.15) | collective-permute-done | bytes 491552 | tf_op jit(solution)/shard_map/ppermute | solution.py:17
  306.1 10.1 %constant_dynamic-update-slice_fusion.5 = (bf16[16,271,256]{2,1,0:T(8,128)(2,1)S(1)}, bf16[16,64,256]{2,1,0:T(8,128)(2,1)S(1)}) fusion(bf16[16,271,256]{2,1,0:T(8,128)(2,1)S(1)} %get-tuple-element.186, bf16[15,64,256]{2,1,0:T(8,128)(2,1)} %collective-permute-done.16, bf16[16,64,256]{2,1,0:T(8,128)(2,1)} %bitcast.477, f32[256]{0:T(256)S(1)} %bitcast.591, ...), kind=kLoop, calls=%fused_computation.1566 | loop fusion | flops 47972352 | bytes 2587648
  316.3 4.8 %constant_dynamic-update-slice_fusion.4 = (bf16[16,271,256]{2,1,0:T(8,128)(2,1)S(1)}, bf16[16,64,256]{2,1,0:T(8,128)(2,1)S(1)}) fusion(bf16[16,271,256]{2,1,0:T(8,128)(2,1)S(1)} %get-tuple-element.184, bf16[15,64,256]{2,1,0:T(8,128)(2,1)S(1)} %collective-permute-done.18, bf16[16,64,256]{2,1,0:T(8,128)(2,1)S(1)} %bitcast.480, f32[256]{0:T(256)S(1)} %bitcast.592, ...), kind=kLoop, calls=%fused_computation.1565 | loop fusion | flops 47972352 | bytes 2587648
  321.1 8.4 %constant_dynamic-update-slice_fusion.3 = (bf16[16,271,256]{2,1,0:T(8,128)(2,1)S(1)}, bf16[16,64,256]{2,1,0:T(8,128)(2,1)S(1)}) fusion(bf16[16,271,256]{2,1,0:T(8,128)(2,1)S(1)} %get-tuple-element.182, bf16[15,64,256]{2,1,0:T(8,128)(2,1)} %collective-permute-done.11, bf16[16,64,256]{2,1,0:T(8,128)(2,1)S(1)} %bitcast.476, f32[256]{0:T(256)S(1)} %bitcast.593, ...), kind=kLoop, calls=%fused_computation.1564 | loop fusion | flops 47972352 | bytes 2587648
  329.6 3.8 fusion.69
  333.3 3.5 fusion.66
  342.8 2.7 fusion.50
  347.9 3.7 fusion.71
  351.9 3.9 convolution_add_fusion.3
  358.1 3.7 collective-permute-start.12
  365.7 7.3 %concatenate.385 = bf16[16,271,256]{2,1,0:T(8,128)(2,1)S(1)} concatenate(bf16[16,15,256]{2,1,0:T(8,128)(2,1)S(1)} %collective-permute-done.12, bf16[16,64,256]{2,1,0:T(8,128)(2,1)S(1)} %get-tuple-element.187, bf16[16,64,256]{2,1,0:T(8,128)(2,1)} %copy-done.7, bf16[16,64,256]{2,1,0:T(8,128)(2,1)} %copy-done.8, bf16[16,64,256]{2,1,0:T(8,128)(2,1)S(1)} %get-tuple-element.181), dimensions={1} | concatenate | bytes 4440064 | tf_op jit(solution)/shard_map/concatenate | solution.py:19
  380.9 30.1 %fusion.72 = bf16[16,256,256]{2,1,0:T(8,128)(2,1)} fusion(bf16[16,271,256]{2,1,0:T(8,128)(2,1)} %constant_dynamic-update-slice_fusion.2, bf16[16,271,256]{2,1,0:T(8,128)(2,1)S(1)} %concatenate.385, bf16[16,64,256]{2,1,0:T(8,128)(2,1)} %bitcast.475, bf16[16,64,256]{2,1,0:T(8,128)(2,1)} %bitcast.479, bf16[16,64,256]{2,1,0:T(8,128)(2,1)} %bitcast.478, ...), kind=kLoop, calls=%fused_computation.273 | loop fusion | flops 114294784 | bytes 69237760 | tf_op jit(solution)/shard_map/convert_element_type | solution.py:143
  412.2 45.8 %all-reduce.3.cloned.1.call-done = (f32[256,1024]{1,0:T(8,128)}, f32[1024,256]{1,0:T(8,128)}) async-done(((f32[256,1024]{1,0:T(8,128)}, f32[1024,256]{1,0:T(8,128)}), (f32[256,1024]{1,0:T(8,128)}, f32[1024,256]{1,0:T(8,128)})) %all-reduce.3.cloned.1.call-update) | async-done | bytes 2097168 | tf_op jit(solution)/shard_map/psum | solution.py:138
  (283 shorter events, 107.5 us)
Async XLA Ops:
  7.2 131.7 %copy-start = (bf16[256,1024]{1,0:T(8,128)(2,1)S(1)}, bf16[256,1024]{1,0:T(8,128)(2,1)}, u32[]{:S(2)}) copy-start(bf16[256,1024]{1,0:T(8,128)(2,1)} %param.12) | copy-start | bytes 1572868
  7.2 450.8 %all-reduce.3.cloned.1.call-start = ((), (), s32[]{:S(2)}) async-start(), calls=%async_computation | async-start | bytes 4194304 | tf_op jit(solution)/shard_map/psum | solution.py:138
  8.3 36.0 %collective-permute-start = (bf16[16,15,256]{2,1,0:T(8,128)(2,1)S(1)}, bf16[16,15,256]{2,1,0:T(8,128)(2,1)S(1)}, u32[]{:S(2)}, u32[]{:S(2)}) collective-permute-start(bf16[16,15,256]{2,1,0:T(8,128)(2,1)S(1)} %get-tuple-element.212), channel_id=1, source_target_pairs={{0,1},{2,3},{4,5},{6,7},{8,9},{10,11},{12,13},{14,15},{16,17},{18,... | collective-permute-start | bytes 368648 | tf_op jit(solution)/shard_map/ppermute | solution.py:17
  10.7 40.7 %collective-permute-start.7 = (bf16[16,15,256]{2,1,0:T(8,128)(2,1)S(1)}, bf16[16,15,256]{2,1,0:T(8,128)(2,1)S(1)}, u32[]{:S(2)}, u32[]{:S(2)}) collective-permute-start(bf16[16,15,256]{2,1,0:T(8,128)(2,1)S(1)} %get-tuple-element.213), channel_id=1, source_target_pairs={{1,0},{3,2},{5,4},{7,6},{9,8},{11,10},{13,12},{15,14},{17,16},{19,... | collective-permute-start | bytes 368648 | tf_op jit(solution)/shard_map/ppermute | solution.py:18
  13.0 44.4 %copy-start.50 = (f32[1,256]{1,0:T(1,128)}, f32[1,256]{1,0:T(1,128)S(1)}, u32[]{:S(2)}) copy-start(f32[1,256]{1,0:T(1,128)S(1)} %get-tuple-element.294) | copy-start | bytes 3076
  13.0 44.4 %copy-start.51 = (f32[1,256]{1,0:T(1,128)}, f32[1,256]{1,0:T(1,128)S(1)}, u32[]{:S(2)}) copy-start(f32[1,256]{1,0:T(1,128)S(1)} %get-tuple-element.295) | copy-start | bytes 3076
  13.0 44.4 %copy-start.52 = (f32[1,256]{1,0:T(1,128)}, f32[1,256]{1,0:T(1,128)S(1)}, u32[]{:S(2)}) copy-start(f32[1,256]{1,0:T(1,128)S(1)} %get-tuple-element.296) | copy-start | bytes 3076
  13.0 44.4 %copy-start.53 = (f32[1,256]{1,0:T(1,128)}, f32[1,256]{1,0:T(1,128)S(1)}, u32[]{:S(2)}) copy-start(f32[1,256]{1,0:T(1,128)S(1)} %get-tuple-element.297) | copy-start | bytes 3076
  13.0 44.4 %copy-start.54 = (f32[1,256]{1,0:T(1,128)}, f32[1,256]{1,0:T(1,128)S(1)}, u32[]{:S(2)}) copy-start(f32[1,256]{1,0:T(1,128)S(1)} %get-tuple-element.298) | copy-start | bytes 3076
  13.0 44.4 %copy-start.55 = (f32[1,256]{1,0:T(1,128)}, f32[1,256]{1,0:T(1,128)S(1)}, u32[]{:S(2)}) copy-start(f32[1,256]{1,0:T(1,128)S(1)} %get-tuple-element.299) | copy-start | bytes 3076
  13.0 44.4 %copy-start.56 = (f32[1,256]{1,0:T(1,128)}, f32[1,256]{1,0:T(1,128)S(1)}, u32[]{:S(2)}) copy-start(f32[1,256]{1,0:T(1,128)S(1)} %get-tuple-element.300) | copy-start | bytes 3076
  13.1 44.4 %copy-start.57 = (f32[1,256]{1,0:T(1,128)}, f32[1,256]{1,0:T(1,128)S(1)}, u32[]{:S(2)}) copy-start(f32[1,256]{1,0:T(1,128)S(1)} %get-tuple-element.301) | copy-start | bytes 3076
  14.1 43.4 %copy-start.58 = (f32[1,256]{1,0:T(1,128)}, f32[1,256]{1,0:T(1,128)S(1)}, u32[]{:S(2)}) copy-start(f32[1,256]{1,0:T(1,128)S(1)} %get-tuple-element.271) | copy-start | bytes 3076
  14.1 43.4 %copy-start.59 = (f32[1,256]{1,0:T(1,128)}, f32[1,256]{1,0:T(1,128)S(1)}, u32[]{:S(2)}) copy-start(f32[1,256]{1,0:T(1,128)S(1)} %get-tuple-element.272) | copy-start | bytes 3076
  14.1 43.4 %copy-start.60 = (f32[1,256]{1,0:T(1,128)}, f32[1,256]{1,0:T(1,128)S(1)}, u32[]{:S(2)}) copy-start(f32[1,256]{1,0:T(1,128)S(1)} %get-tuple-element.273) | copy-start | bytes 3076
  14.1 43.4 %copy-start.61 = (f32[1,256]{1,0:T(1,128)}, f32[1,256]{1,0:T(1,128)S(1)}, u32[]{:S(2)}) copy-start(f32[1,256]{1,0:T(1,128)S(1)} %get-tuple-element.274) | copy-start | bytes 3076
  14.1 43.4 %copy-start.62 = (f32[1,256]{1,0:T(1,128)}, f32[1,256]{1,0:T(1,128)S(1)}, u32[]{:S(2)}) copy-start(f32[1,256]{1,0:T(1,128)S(1)} %get-tuple-element.275) | copy-start | bytes 3076
  14.1 43.4 %copy-start.63 = (f32[1,256]{1,0:T(1,128)}, f32[1,256]{1,0:T(1,128)S(1)}, u32[]{:S(2)}) copy-start(f32[1,256]{1,0:T(1,128)S(1)} %get-tuple-element.276) | copy-start | bytes 3076
  14.1 43.4 %copy-start.64 = (f32[1,256]{1,0:T(1,128)}, f32[1,256]{1,0:T(1,128)S(1)}, u32[]{:S(2)}) copy-start(f32[1,256]{1,0:T(1,128)S(1)} %get-tuple-element.277) | copy-start | bytes 3076
  14.2 43.4 %copy-start.65 = (f32[1,256]{1,0:T(1,128)}, f32[1,256]{1,0:T(1,128)S(1)}, u32[]{:S(2)}) copy-start(f32[1,256]{1,0:T(1,128)S(1)} %get-tuple-element.278) | copy-start | bytes 3076
  27.8 61.2 %copy-start.21 = (bf16[16,64,256]{2,1,0:T(8,128)(2,1)}, bf16[16,64,256]{2,1,0:T(8,128)(2,1)S(1)}, u32[]{:S(2)}) copy-start(bf16[16,64,256]{2,1,0:T(8,128)(2,1)S(1)} %fusion.472) | copy-start | bytes 1572868
  27.9 59.8 %collective-permute-start.5 = (bf16[15,64,256]{2,1,0:T(8,128)(2,1)S(1)}, bf16[15,64,256]{2,1,0:T(8,128)(2,1)S(1)}, u32[]{:S(2)}, u32[]{:S(2)}) collective-permute-start(bf16[15,64,256]{2,1,0:T(8,128)(2,1)S(1)} %get-tuple-element.234), channel_id=1, source_target_pairs={{0,2},{2,4},{4,6},{6,8},{8,10},{10,12},{12,14},{1,3},{3,5},{5,7},{... | collective-permute-start | bytes 1474568 | tf_op jit(solution)/shard_map/ppermute | solution.py:17
  32.2 56.8 %collective-permute-start.6 = (bf16[15,64,256]{2,1,0:T(8,128)(2,1)S(1)}, bf16[15,64,256]{2,1,0:T(8,128)(2,1)S(1)}, u32[]{:S(2)}, u32[]{:S(2)}) collective-permute-start(bf16[15,64,256]{2,1,0:T(8,128)(2,1)S(1)} %get-tuple-element.235), channel_id=1, source_target_pairs={{2,0},{4,2},{6,4},{8,6},{10,8},{12,10},{14,12},{3,1},{5,3},{7,5},{... | collective-permute-start | bytes 1474568 | tf_op jit(solution)/shard_map/ppermute | solution.py:18
  38.1 44.2 %copy-start.18 = (bf16[16,64,256]{2,1,0:T(8,128)(2,1)}, bf16[16,64,256]{2,1,0:T(8,128)(2,1)S(1)}, u32[]{:S(2)}) copy-start(bf16[16,64,256]{2,1,0:T(8,128)(2,1)S(1)} %fusion.473) | copy-start | bytes 1572868
  38.2 37.0 %collective-permute-start.3 = (bf16[15,64,256]{2,1,0:T(8,128)(2,1)S(1)}, bf16[15,64,256]{2,1,0:T(8,128)(2,1)S(1)}, u32[]{:S(2)}, u32[]{:S(2)}) collective-permute-start(bf16[15,64,256]{2,1,0:T(8,128)(2,1)S(1)} %get-tuple-element.232), channel_id=1, source_target_pairs={{0,2},{2,4},{4,6},{6,8},{8,10},{10,12},{12,14},{1,3},{3,5},{5,7},{... | collective-permute-start | bytes 1474568 | tf_op jit(solution)/shard_map/ppermute | solution.py:17
  44.3 32.1 %collective-permute-start.4 = (bf16[15,64,256]{2,1,0:T(8,128)(2,1)S(1)}, bf16[15,64,256]{2,1,0:T(8,128)(2,1)S(1)}, u32[]{:S(2)}, u32[]{:S(2)}) collective-permute-start(bf16[15,64,256]{2,1,0:T(8,128)(2,1)S(1)} %get-tuple-element.233), channel_id=1, source_target_pairs={{2,0},{4,2},{6,4},{8,6},{10,8},{12,10},{14,12},{3,1},{5,3},{7,5},{... | collective-permute-start | bytes 1474568 | tf_op jit(solution)/shard_map/ppermute | solution.py:18
  51.5 45.3 %collective-permute-start.1 = (bf16[15,64,256]{2,1,0:T(8,128)(2,1)}, bf16[15,64,256]{2,1,0:T(8,128)(2,1)}, u32[]{:S(2)}, u32[]{:S(2)}) collective-permute-start(bf16[15,64,256]{2,1,0:T(8,128)(2,1)} %get-tuple-element.230), channel_id=1, source_target_pairs={{0,2},{2,4},{4,6},{6,8},{8,10},{10,12},{12,14},{1,3},{3,5},{5,7},{... | collective-permute-start | bytes 1474568 | tf_op jit(solution)/shard_map/ppermute | solution.py:17
  62.1 55.3 %copy-start.23 = (bf16[16,64,256]{2,1,0:T(8,128)(2,1)}, bf16[16,64,256]{2,1,0:T(8,128)(2,1)S(1)}, u32[]{:S(2)}) copy-start(bf16[16,64,256]{2,1,0:T(8,128)(2,1)S(1)} %fusion.471) | copy-start | bytes 1572868
  75.2 21.6 %collective-permute-start.2 = (bf16[15,64,256]{2,1,0:T(8,128)(2,1)}, bf16[15,64,256]{2,1,0:T(8,128)(2,1)}, u32[]{:S(2)}, u32[]{:S(2)}) collective-permute-start(bf16[15,64,256]{2,1,0:T(8,128)(2,1)} %get-tuple-element.231), channel_id=1, source_target_pairs={{2,0},{4,2},{6,4},{8,6},{10,8},{12,10},{14,12},{3,1},{5,3},{7,5},{... | collective-permute-start | bytes 1474568 | tf_op jit(solution)/shard_map/ppermute | solution.py:18
  76.5 40.9 %collective-permute-start.8 = (bf16[15,64,256]{2,1,0:T(8,128)(2,1)}, bf16[15,64,256]{2,1,0:T(8,128)(2,1)}, u32[]{:S(2)}, u32[]{:S(2)}) collective-permute-start(bf16[15,64,256]{2,1,0:T(8,128)(2,1)} %get-tuple-element.236), channel_id=1, source_target_pairs={{0,2},{2,4},{4,6},{6,8},{8,10},{10,12},{12,14},{1,3},{3,5},{5,7},{... | collective-permute-start | bytes 1474568 | tf_op jit(solution)/shard_map/ppermute | solution.py:17
  87.7 29.7 %collective-permute-start.9 = (bf16[15,64,256]{2,1,0:T(8,128)(2,1)}, bf16[15,64,256]{2,1,0:T(8,128)(2,1)}, u32[]{:S(2)}, u32[]{:S(2)}) collective-permute-start(bf16[15,64,256]{2,1,0:T(8,128)(2,1)} %get-tuple-element.237), channel_id=1, source_target_pairs={{2,0},{4,2},{6,4},{8,6},{10,8},{12,10},{14,12},{3,1},{5,3},{7,5},{... | collective-permute-start | bytes 1474568 | tf_op jit(solution)/shard_map/ppermute | solution.py:18
  175.2 66.9 %copy-start.11 = (bf16[1024,256]{1,0:T(8,128)(2,1)}, bf16[1024,256]{1,0:T(8,128)(2,1)S(1)}, u32[]{:S(2)}) copy-start(bf16[1024,256]{1,0:T(8,128)(2,1)S(1)} %get-tuple-element.179) | copy-start | bytes 1572868
  176.3 102.6 %collective-permute-start.14 = (bf16[15,64,256]{2,1,0:T(8,128)(2,1)}, bf16[15,64,256]{2,1,0:T(8,128)(2,1)}, u32[]{:S(2)}, u32[]{:S(2)}) collective-permute-start(bf16[15,64,256]{2,1,0:T(8,128)(2,1)} %bitcast.81), channel_id=1, source_target_pairs={{2,0},{4,2},{6,4},{8,6},{10,8},{12,10},{14,12},{3,1},{5,3},{7,5},{... | collective-permute-start | bytes 1474568 | tf_op jit(solution)/shard_map/ppermute | solution.py:18
  177.6 106.2 %collective-permute-start.13 = (bf16[15,64,256]{2,1,0:T(8,128)(2,1)}, bf16[15,64,256]{2,1,0:T(8,128)(2,1)}, u32[]{:S(2)}, u32[]{:S(2)}) collective-permute-start(bf16[15,64,256]{2,1,0:T(8,128)(2,1)} %bitcast.80), channel_id=1, source_target_pairs={{0,2},{2,4},{4,6},{6,8},{8,10},{10,12},{12,14},{1,3},{3,5},{5,7},{... | collective-permute-start | bytes 1474568 | tf_op jit(solution)/shard_map/ppermute | solution.py:17
  191.3 129.9 %collective-permute-start.11 = (bf16[15,64,256]{2,1,0:T(8,128)(2,1)}, bf16[15,64,256]{2,1,0:T(8,128)(2,1)}, u32[]{:S(2)}, u32[]{:S(2)}) collective-permute-start(bf16[15,64,256]{2,1,0:T(8,128)(2,1)} %bitcast.79), channel_id=1, source_target_pairs={{2,0},{4,2},{6,4},{8,6},{10,8},{12,10},{14,12},{3,1},{5,3},{7,5},{... | collective-permute-start | bytes 1474568 | tf_op jit(solution)/shard_map/ppermute | solution.py:18
  192.6 128.6 %collective-permute-start.10 = (bf16[15,64,256]{2,1,0:T(8,128)(2,1)}, bf16[15,64,256]{2,1,0:T(8,128)(2,1)}, u32[]{:S(2)}, u32[]{:S(2)}) collective-permute-start(bf16[15,64,256]{2,1,0:T(8,128)(2,1)} %bitcast.78), channel_id=1, source_target_pairs={{0,2},{2,4},{4,6},{6,8},{8,10},{10,12},{12,14},{1,3},{3,5},{5,7},{... | collective-permute-start | bytes 1474568 | tf_op jit(solution)/shard_map/ppermute | solution.py:17
  218.1 43.7 %copy-start.15 = (bf16[1024,256]{1,0:T(8,128)(2,1)}, bf16[1024,256]{1,0:T(8,128)(2,1)S(1)}, u32[]{:S(2)}) copy-start(bf16[1024,256]{1,0:T(8,128)(2,1)S(1)} %get-tuple-element.177) | copy-start | bytes 1572868
  219.2 73.8 %collective-permute-start.16 = (bf16[15,64,256]{2,1,0:T(8,128)(2,1)}, bf16[15,64,256]{2,1,0:T(8,128)(2,1)}, u32[]{:S(2)}, u32[]{:S(2)}) collective-permute-start(bf16[15,64,256]{2,1,0:T(8,128)(2,1)} %bitcast.83), channel_id=1, source_target_pairs={{2,0},{4,2},{6,4},{8,6},{10,8},{12,10},{14,12},{3,1},{5,3},{7,5},{... | collective-permute-start | bytes 1474568 | tf_op jit(solution)/shard_map/ppermute | solution.py:18
  278.9 27.2 %collective-permute-start.15 = (bf16[15,64,256]{2,1,0:T(8,128)(2,1)}, bf16[15,64,256]{2,1,0:T(8,128)(2,1)S(1)}, u32[]{:S(2)}, u32[]{:S(2)}) collective-permute-start(bf16[15,64,256]{2,1,0:T(8,128)(2,1)} %bitcast.487), channel_id=1, source_target_pairs={{0,2},{2,4},{4,6},{6,8},{8,10},{10,12},{12,14},{1,3},{3,5},{5,7},{... | collective-permute-start | bytes 1474568 | tf_op jit(solution)/shard_map/ppermute | solution.py:17
  283.7 32.5 %collective-permute-start.18 = (bf16[15,64,256]{2,1,0:T(8,128)(2,1)}, bf16[15,64,256]{2,1,0:T(8,128)(2,1)S(1)}, u32[]{:S(2)}, u32[]{:S(2)}) collective-permute-start(bf16[15,64,256]{2,1,0:T(8,128)(2,1)} %bitcast.489), channel_id=1, source_target_pairs={{2,0},{4,2},{6,4},{8,6},{10,8},{12,10},{14,12},{3,1},{5,3},{7,5},{... | collective-permute-start | bytes 1474568 | tf_op jit(solution)/shard_map/ppermute | solution.py:18
  293.0 23.3 %collective-permute-start.17 = (bf16[15,64,256]{2,1,0:T(8,128)(2,1)}, bf16[15,64,256]{2,1,0:T(8,128)(2,1)S(1)}, u32[]{:S(2)}, u32[]{:S(2)}) collective-permute-start(bf16[15,64,256]{2,1,0:T(8,128)(2,1)} %bitcast.488), channel_id=1, source_target_pairs={{0,2},{2,4},{4,6},{6,8},{8,10},{10,12},{12,14},{1,3},{3,5},{5,7},{... | collective-permute-start | bytes 1474568 | tf_op jit(solution)/shard_map/ppermute | solution.py:17
  351.9 9.9 %collective-permute-start.20 = (f32[63,256]{1,0:T(8,128)S(1)}, f32[63,256]{1,0:T(8,128)S(1)}, u32[]{:S(2)}, u32[]{:S(2)}) collective-permute-start(f32[63,256]{1,0:T(8,128)S(1)} %concatenate.388), channel_id=1, source_target_pairs={{0,1},{1,0},{2,3},{3,2},{4,5},{5,4},{6,7},{7,6},{8,9},{9,8},{10,11... | collective-permute-start | bytes 193544 | tf_op jit(solution)/shard_map/ppermute | solution.py:55
  356.6 18.3 %collective-permute-start.19 = (bf16[16,15,256]{2,1,0:T(8,128)(2,1)}, bf16[16,15,256]{2,1,0:T(8,128)(2,1)}, u32[]{:S(2)}, u32[]{:S(2)}) collective-permute-start(bf16[16,15,256]{2,1,0:T(8,128)(2,1)} %slice.3598), channel_id=1, source_target_pairs={{1,0},{3,2},{5,4},{7,6},{9,8},{11,10},{13,12},{15,14},{17,16},{19,... | collective-permute-start | bytes 368648 | tf_op jit(solution)/shard_map/ppermute | solution.py:18
  358.1 7.6 %collective-permute-start.12 = (bf16[16,15,256]{2,1,0:T(8,128)(2,1)S(1)}, bf16[16,15,256]{2,1,0:T(8,128)(2,1)S(1)}, u32[]{:S(2)}, u32[]{:S(2)}) collective-permute-start(bf16[16,15,256]{2,1,0:T(8,128)(2,1)S(1)} %slice.3408), channel_id=1, source_target_pairs={{0,1},{2,3},{4,5},{6,7},{8,9},{10,11},{12,13},{14,15},{16,17},{18,... | collective-permute-start | bytes 368648 | tf_op jit(solution)/shard_map/ppermute | solution.py:17
  361.8 11.3 %collective-permute-start.21 = (f32[63,256]{1,0:T(8,128)S(1)}, f32[63,256]{1,0:T(8,128)S(1)}, u32[]{:S(2)}, u32[]{:S(2)}) collective-permute-start(f32[63,256]{1,0:T(8,128)S(1)} %add.1799), channel_id=1, source_target_pairs={{0,2},{2,0},{4,6},{6,4},{8,10},{10,8},{12,14},{14,12},{1,3},{3,1},... | collective-permute-start | bytes 193544 | tf_op jit(solution)/shard_map/ppermute | solution.py:55
  373.1 5.2 %collective-permute-start.22 = (f32[63,256]{1,0:T(8,128)S(1)}, f32[63,256]{1,0:T(8,128)S(1)}, u32[]{:S(2)}, u32[]{:S(2)}) collective-permute-start(f32[63,256]{1,0:T(8,128)S(1)} %add.1800), channel_id=1, source_target_pairs={{0,4},{2,6},{4,0},{6,2},{8,12},{10,14},{12,8},{14,10},{1,5},{3,7},... | collective-permute-start | bytes 193544 | tf_op jit(solution)/shard_map/ppermute | solution.py:55
  378.3 32.7 %collective-permute-start.23 = (f32[63,256]{1,0:T(8,128)S(1)}, f32[63,256]{1,0:T(8,128)S(1)}, u32[]{:S(2)}, u32[]{:S(2)}) collective-permute-start(f32[63,256]{1,0:T(8,128)S(1)} %add.1801), channel_id=1, source_target_pairs={{0,8},{2,10},{4,12},{6,14},{8,0},{10,2},{12,4},{14,6},{1,9},{3,11}... | collective-permute-start | bytes 193544 | tf_op jit(solution)/shard_map/ppermute | solution.py:55
  380.9 81.7 %copy-start.1 = (bf16[256,1024]{1,0:T(8,128)(2,1)S(1)}, bf16[256,1024]{1,0:T(8,128)(2,1)}, u32[]{:S(2)}) copy-start(bf16[256,1024]{1,0:T(8,128)(2,1)} %param.12) | copy-start | bytes 1572868
  (56 other events, 1078.0 us)
Sparse Core Ops, SparseCore 0:
  356.0 101.9 all-reduce.2
